TPU v7x, 768 devices: a whole 4x8x12 slice. The times are simulated.
768 devices in a mesh: dp: 12 (over z), phase: 4 (over x), ctx: 16 (over y, core).
Axes of the slice: x: 4, y: 8, z: 12, core: 2. Of those that a mesh axis runs over, the one named last changes fastest.
Arguments:
- queries: bfloat16 [12, 4096, 4096], P('dp', 'ctx', 'phase'), may hold values from -6 to 6
- keys: bfloat16 [12, 4096, 512], P('dp', 'ctx', 'phase'), may hold values from -6 to 6
- values: bfloat16 [12, 4096, 512], P('dp', 'ctx', 'phase'), may hold values from -6 to 6
- segment_ids: int32 [12, 4096], P('dp', 'ctx'), may hold values from 0 to 7, never falling along the last dimension, each value on 1 to 1024 neighbouring positions
- span_ids: int32 [12, 4096], P('dp', 'ctx'), may hold values from 0 to 2, as said below
- readout: float32 [4096], P('phase'), may hold values from -6 to 6
Outputs:
- attended: bfloat16 [12, 4096, 4096], P('dp', 'ctx', 'phase')
- span_scores: float32 [12, 2], P('dp')
- pair_loss: float32 [], replicated
Inputs may be any that keep to these rules, and one draw needn't show every extreme that they name: `segment_ids`: segment ids never fall along a sequence; each segment covers at most 1024 positions, and some segment covers exactly that many. `span_ids`: positions labelled 1 form one contiguous run, and positions labelled 2 form one later contiguous run.
All inputs are finite; a program needn't handle non-finite values.
Results may differ from a plain program's by a relative error of at most 0.0036.
Values may be sent and summed in bfloat16 or wider, within the bound.
No kernel may reach another device: no remote copies, remote signals or barrier semaphores. Data moves between devices by JAX's collectives and lax.ppermute only.
A program may use at most 128 MiB of HBM per device.

v0:
```python
import jax
import jax.numpy as jnp
from jax import lax
from jax.sharding import PartitionSpec as P


def passed_along(array, axis, by):
    devices = lax.axis_size(axis)
    pairs = [(i, i + by) for i in range(devices) if 0 <= i + by < devices]
    return lax.ppermute(array, axis, pairs)


def attend_piece(carry, queries, qpos, qseg, kpiece, vpiece, spiece, kstart, valid):
    top, total, acc = carry
    rows = kpiece.shape[0]
    kpos = kstart + jnp.arange(rows)
    allow = (kpos[None, :] <= qpos[:, None]) & (spiece[None, :] == qseg[:, None]) & valid
    sc = jnp.einsum("hid,jd->hij", queries, kpiece, preferred_element_type=jnp.float32)
    sc = jnp.where(allow[None], sc / jnp.sqrt(jnp.float32(kpiece.shape[1])), jnp.float32(-1e30))
    new_top = jnp.maximum(top, jnp.max(sc, axis=-1))
    prob = jnp.where(allow[None], jnp.exp(sc - new_top[:, :, None]), 0.0)
    scale = jnp.exp(top - new_top)
    total = total * scale + jnp.sum(prob, axis=-1)
    part = jnp.einsum(
        "hij,jd->hid", prob.astype(jnp.bfloat16), vpiece, preferred_element_type=jnp.float32
    )
    return (new_top, total, acc * scale[:, :, None] + part)


def per_device(queries, keys, values, segment_ids, span_ids, readout):
    tok = queries.shape[1]
    head_dim = keys.shape[2]
    heads = queries.shape[2] // head_dim
    here = lax.axis_index("ctx")
    qpos = here * tok + jnp.arange(tok)
    qseg = segment_ids[0]
    qh = jnp.transpose(queries[0].reshape(tok, heads, head_dim), (1, 0, 2))
    init = (
        jnp.full((heads, tok), -1e30, jnp.float32),
        jnp.zeros((heads, tok), jnp.float32),
        jnp.zeros((heads, tok, head_dim), jnp.float32),
    )
    first = attend_piece(init, qh, qpos, qseg, keys[0], values[0], qseg, here * tok, True)

    def near_step(step, state):
        carry, kcur, vcur, scur = state
        kcur, vcur, scur = passed_along((kcur, vcur, scur), "ctx", 1)
        carry = attend_piece(
            carry, qh, qpos, qseg, kcur, vcur, scur, (here - step) * tok, step <= here
        )
        return (carry, kcur, vcur, scur)

    top, total, acc = lax.fori_loop(
        1, lax.axis_size("ctx") // 4 + 1, near_step, (first, keys[0], values[0], qseg)
    )[0]
    full = acc / total[:, :, None]
    flat = jnp.transpose(full, (1, 0, 2)).reshape(tok, heads * head_dim)
    attended = flat.astype(jnp.bfloat16)[None]
    score = jnp.sum(flat * readout[None, :], axis=1)
    spans = span_ids[0]
    partial_value = (
        jnp.stack(
            [jnp.sum(jnp.where(spans == 1, score, 0.0)), jnp.sum(jnp.where(spans == 2, score, 0.0))]
        )
        / 64.0
    )
    span_scores = lax.psum(partial_value, ("phase", "ctx"))
    loss_term = jax.nn.softplus(-(span_scores[0] - span_scores[1]))
    pair_loss = lax.psum(loss_term, "dp") / lax.axis_size("dp")
    return (attended, span_scores[None], pair_loss)


def solution(mesh):
    in_specs = (
        P("dp", "ctx", "phase"),
        P("dp", "ctx", "phase"),
        P("dp", "ctx", "phase"),
        P("dp", "ctx"),
        P("dp", "ctx"),
        P("phase"),
    )
    out_specs = (P("dp", "ctx", "phase"), P("dp", None), P())
    return jax.shard_map(
        per_device, mesh=mesh, in_specs=in_specs, out_specs=out_specs, check_vma=False
    )
```

profile of v0, /device:TPU:1, one launch (start us, length us, event | category | flops | bytes accessed | tf_op | source)
XLA Modules:
  0.0 214.9 jit_solution(10932804182884185317)
XLA Ops:
  0.6 0.8 copy.45
  1.5 0.8 copy.46
  2.3 0.9 compare_and_fusion
  3.2 1.2 copy.13
  4.9 0.5 fusion.19
  5.5 1.0 convolution_add_fusion.1
  6.8 50.3 %while.24 = (s32[]{:T(128)}, f32[8,256]{1,0:T(8,128)S(1)}, f32[8,256]{1,0:T(8,128)S(1)}, f32[8,256,128]{2,1,0:T(8,128)S(1)}, bf16[256,128]{1,0:T(8,128)(2,1)S(1)...) while((s32[]{:T(128)}, f32[8,256]{1,0:T(8,128)S(1)}, ...), condition=%wide.region_5.6_spmd.clone, body=%wide.region_2.5_spmd.clone.sunk | while | flops 276042240 | bytes 10236191 | solution.py:53
  6.8 4.6 %collective-permute-start = (s32[256]{0:T(256)S(1)}, s32[256]{0:T(256)S(1)}, u32[]{:S(2)}, u32[]{:S(2)}) collective-permute-start(s32[256]{0:T(256)S(1)} %get-tuple-element.364), channel_id=1, source_target_pairs={{0,1},{1,2},{2,3},{3,4},{4,5},{5,6},{6,7},{7,8},{8,9},{9,10},{10,1... | collective-permute-start | bytes 3080 | tf_op jit(solution)/shard_map/while/body/eval_jaxpr/ppermute | solution.py:10
  11.4 1.9 collective-permute-start.1
  13.3 3.6 %collective-permute-start.2 = (bf16[256,128]{1,0:T(8,128)(2,1)S(1)}, bf16[256,128]{1,0:T(8,128)(2,1)S(1)}, u32[]{:S(2)}, u32[]{:S(2)}) collective-permute-start(bf16[256,128]{1,0:T(8,128)(2,1)S(1)} %get-tuple-element.363), channel_id=1, source_target_pairs={{0,1},{1,2},{2,3},{3,4},{4,5},{5,6},{6,7},{7,8},{8,9},{9,10},{10,1... | collective-permute-start | bytes 196616 | tf_op jit(solution)/shard_map/while/body/eval_jaxpr/ppermute | solution.py:10
  17.0 2.3 %collective-permute-done = s32[256]{0:T(256)S(1)} collective-permute-done((s32[256]{0:T(256)S(1)}, s32[256]{0:T(256)S(1)}, u32[]{:S(2)}, u32[]{:S(2)}) %collective-permute-start) | collective-permute-done | bytes 1056 | tf_op jit(solution)/shard_map/while/body/eval_jaxpr/ppermute | solution.py:10
  19.4 1.2 collective-permute-done.1
  21.1 0.5 fusion.45
  21.9 1.0 convolution_add_fusion.3
  22.9 1.9 collective-permute-start
  24.8 1.9 collective-permute-start.1
  26.8 2.3 %collective-permute-start.2 = (bf16[256,128]{1,0:T(8,128)(2,1)S(1)}, bf16[256,128]{1,0:T(8,128)(2,1)S(1)}, u32[]{:S(2)}, u32[]{:S(2)}) collective-permute-start(bf16[256,128]{1,0:T(8,128)(2,1)S(1)} %get-tuple-element.363), channel_id=1, source_target_pairs={{0,1},{1,2},{2,3},{3,4},{4,5},{5,6},{6,7},{7,8},{8,9},{9,10},{10,1... | collective-permute-start | bytes 196616 | tf_op jit(solution)/shard_map/while/body/eval_jaxpr/ppermute | solution.py:10
  30.4 1.0 convolution_add_fusion.3
  31.4 4.3 %collective-permute-start = (s32[256]{0:T(256)S(1)}, s32[256]{0:T(256)S(1)}, u32[]{:S(2)}, u32[]{:S(2)}) collective-permute-start(s32[256]{0:T(256)S(1)} %get-tuple-element.364), channel_id=1, source_target_pairs={{0,1},{1,2},{2,3},{3,4},{4,5},{5,6},{6,7},{7,8},{8,9},{9,10},{10,1... | collective-permute-start | bytes 3080 | tf_op jit(solution)/shard_map/while/body/eval_jaxpr/ppermute | solution.py:10
  35.6 2.5 %collective-permute-start.1 = (bf16[256,128]{1,0:T(8,128)(2,1)S(1)}, bf16[256,128]{1,0:T(8,128)(2,1)S(1)}, u32[]{:S(2)}, u32[]{:S(2)}) collective-permute-start(bf16[256,128]{1,0:T(8,128)(2,1)S(1)} %get-tuple-element.362), channel_id=1, source_target_pairs={{0,1},{1,2},{2,3},{3,4},{4,5},{5,6},{6,7},{7,8},{8,9},{9,10},{10,1... | collective-permute-start | bytes 196616 | tf_op jit(solution)/shard_map/while/body/eval_jaxpr/ppermute | solution.py:10
  38.1 4.3 %collective-permute-start.2 = (bf16[256,128]{1,0:T(8,128)(2,1)S(1)}, bf16[256,128]{1,0:T(8,128)(2,1)S(1)}, u32[]{:S(2)}, u32[]{:S(2)}) collective-permute-start(bf16[256,128]{1,0:T(8,128)(2,1)S(1)} %get-tuple-element.363), channel_id=1, source_target_pairs={{0,1},{1,2},{2,3},{3,4},{4,5},{5,6},{6,7},{7,8},{8,9},{9,10},{10,1... | collective-permute-start | bytes 196616 | tf_op jit(solution)/shard_map/while/body/eval_jaxpr/ppermute | solution.py:10
  43.7 1.0 convolution_add_fusion.3
  44.7 4.3 %collective-permute-start = (s32[256]{0:T(256)S(1)}, s32[256]{0:T(256)S(1)}, u32[]{:S(2)}, u32[]{:S(2)}) collective-permute-start(s32[256]{0:T(256)S(1)} %get-tuple-element.364), channel_id=1, source_target_pairs={{0,1},{1,2},{2,3},{3,4},{4,5},{5,6},{6,7},{7,8},{8,9},{9,10},{10,1... | collective-permute-start | bytes 3080 | tf_op jit(solution)/shard_map/while/body/eval_jaxpr/ppermute | solution.py:10
  49.0 1.9 collective-permute-start.1
  50.9 3.9 %collective-permute-start.2 = (bf16[256,128]{1,0:T(8,128)(2,1)S(1)}, bf16[256,128]{1,0:T(8,128)(2,1)S(1)}, u32[]{:S(2)}, u32[]{:S(2)}) collective-permute-start(bf16[256,128]{1,0:T(8,128)(2,1)S(1)} %get-tuple-element.363), channel_id=1, source_target_pairs={{0,1},{1,2},{2,3},{3,4},{4,5},{5,6},{6,7},{7,8},{8,9},{9,10},{10,1... | collective-permute-start | bytes 196616 | tf_op jit(solution)/shard_map/while/body/eval_jaxpr/ppermute | solution.py:10
  56.1 1.0 convolution_add_fusion.3
  57.6 0.6 select_reduce_fusion.1
  58.2 1.4 maximum_multiply_fusion
  59.5 121.9 %psum.14 = f32[2]{0:T(128)S(1)} all-reduce(f32[2]{0:T(128)S(1)} %maximum_multiply_fusion), channel_id=1, replica_groups=mesh['dp'=12,'phase'=4,'ctx'=16] {'phase','ctx'}, use_global_device_ids=true, to_apply=%region_9.10 | all-reduce | flops 2 | bytes 16 | tf_op jit(solution)/shard_map/psum | solution.py:67
  181.4 0.6 fusion.33
  183.4 28.3 %psum.15 = f32[]{:T(128)} all-reduce(f32[]{:T(128)S(6)} %select_n.37), channel_id=1, replica_groups=mesh['dp'=12,'phase'=4,'ctx'=16] {'dp'}, use_global_device_ids=true, to_apply=%region_10.11 | all-reduce | flops 1 | bytes 8 | tf_op jit(solution)/shard_map/psum | solution.py:69
  212.7 1.0 convert_element_type.29
  (66 shorter events, 6.1 us)
Async XLA Ops:
  5.5 1.3 copy-start
  6.8 50.3 %copy-start.1 = (f32[1024]{0:T(1024)S(1)}, f32[1024]{0:T(1024)}, u32[]{:S(2)}) copy-start(f32[1024]{0:T(1024)} %param.13) | copy-start | bytes 12292
  6.8 50.7 %copy-start.3 = (s32[1,256]{1,0:T(1,128)S(1)}, s32[1,256]{1,0:T(1,128)}, u32[]{:S(2)}) copy-start(s32[1,256]{1,0:T(1,128)} %param.12) | copy-start | bytes 3076
  6.8 12.4 %collective-permute-start = (s32[256]{0:T(256)S(1)}, s32[256]{0:T(256)S(1)}, u32[]{:S(2)}, u32[]{:S(2)}) collective-permute-start(s32[256]{0:T(256)S(1)} %get-tuple-element.364), channel_id=1, source_target_pairs={{0,1},{1,2},{2,3},{3,4},{4,5},{5,6},{6,7},{7,8},{8,9},{9,10},{10,1... | collective-permute-start | bytes 3080 | tf_op jit(solution)/shard_map/while/body/eval_jaxpr/ppermute | solution.py:10
  11.4 9.2 %collective-permute-start.1 = (bf16[256,128]{1,0:T(8,128)(2,1)S(1)}, bf16[256,128]{1,0:T(8,128)(2,1)S(1)}, u32[]{:S(2)}, u32[]{:S(2)}) collective-permute-start(bf16[256,128]{1,0:T(8,128)(2,1)S(1)} %get-tuple-element.362), channel_id=1, source_target_pairs={{0,1},{1,2},{2,3},{3,4},{4,5},{5,6},{6,7},{7,8},{8,9},{9,10},{10,1... | collective-permute-start | bytes 196616 | tf_op jit(solution)/shard_map/while/body/eval_jaxpr/ppermute | solution.py:10
  13.3 8.6 %collective-permute-start.2 = (bf16[256,128]{1,0:T(8,128)(2,1)S(1)}, bf16[256,128]{1,0:T(8,128)(2,1)S(1)}, u32[]{:S(2)}, u32[]{:S(2)}) collective-permute-start(bf16[256,128]{1,0:T(8,128)(2,1)S(1)} %get-tuple-element.363), channel_id=1, source_target_pairs={{0,1},{1,2},{2,3},{3,4},{4,5},{5,6},{6,7},{7,8},{8,9},{9,10},{10,1... | collective-permute-start | bytes 196616 | tf_op jit(solution)/shard_map/while/body/eval_jaxpr/ppermute | solution.py:10
  22.9 6.1 %collective-permute-start = (s32[256]{0:T(256)S(1)}, s32[256]{0:T(256)S(1)}, u32[]{:S(2)}, u32[]{:S(2)}) collective-permute-start(s32[256]{0:T(256)S(1)} %get-tuple-element.364), channel_id=1, source_target_pairs={{0,1},{1,2},{2,3},{3,4},{4,5},{5,6},{6,7},{7,8},{8,9},{9,10},{10,1... | collective-permute-start | bytes 3080 | tf_op jit(solution)/shard_map/while/body/eval_jaxpr/ppermute | solution.py:10
  24.8 4.4 %collective-permute-start.1 = (bf16[256,128]{1,0:T(8,128)(2,1)S(1)}, bf16[256,128]{1,0:T(8,128)(2,1)S(1)}, u32[]{:S(2)}, u32[]{:S(2)}) collective-permute-start(bf16[256,128]{1,0:T(8,128)(2,1)S(1)} %get-tuple-element.362), channel_id=1, source_target_pairs={{0,1},{1,2},{2,3},{3,4},{4,5},{5,6},{6,7},{7,8},{8,9},{9,10},{10,1... | collective-permute-start | bytes 196616 | tf_op jit(solution)/shard_map/while/body/eval_jaxpr/ppermute | solution.py:10
  26.8 3.6 %collective-permute-start.2 = (bf16[256,128]{1,0:T(8,128)(2,1)S(1)}, bf16[256,128]{1,0:T(8,128)(2,1)S(1)}, u32[]{:S(2)}, u32[]{:S(2)}) collective-permute-start(bf16[256,128]{1,0:T(8,128)(2,1)S(1)} %get-tuple-element.363), channel_id=1, source_target_pairs={{0,1},{1,2},{2,3},{3,4},{4,5},{5,6},{6,7},{7,8},{8,9},{9,10},{10,1... | collective-permute-start | bytes 196616 | tf_op jit(solution)/shard_map/while/body/eval_jaxpr/ppermute | solution.py:10
  31.4 11.0 %collective-permute-start = (s32[256]{0:T(256)S(1)}, s32[256]{0:T(256)S(1)}, u32[]{:S(2)}, u32[]{:S(2)}) collective-permute-start(s32[256]{0:T(256)S(1)} %get-tuple-element.364), channel_id=1, source_target_pairs={{0,1},{1,2},{2,3},{3,4},{4,5},{5,6},{6,7},{7,8},{8,9},{9,10},{10,1... | collective-permute-start | bytes 3080 | tf_op jit(solution)/shard_map/while/body/eval_jaxpr/ppermute | solution.py:10
  35.6 6.9 %collective-permute-start.1 = (bf16[256,128]{1,0:T(8,128)(2,1)S(1)}, bf16[256,128]{1,0:T(8,128)(2,1)S(1)}, u32[]{:S(2)}, u32[]{:S(2)}) collective-permute-start(bf16[256,128]{1,0:T(8,128)(2,1)S(1)} %get-tuple-element.362), channel_id=1, source_target_pairs={{0,1},{1,2},{2,3},{3,4},{4,5},{5,6},{6,7},{7,8},{8,9},{9,10},{10,1... | collective-permute-start | bytes 196616 | tf_op jit(solution)/shard_map/while/body/eval_jaxpr/ppermute | solution.py:10
  38.1 5.6 %collective-permute-start.2 = (bf16[256,128]{1,0:T(8,128)(2,1)S(1)}, bf16[256,128]{1,0:T(8,128)(2,1)S(1)}, u32[]{:S(2)}, u32[]{:S(2)}) collective-permute-start(bf16[256,128]{1,0:T(8,128)(2,1)S(1)} %get-tuple-element.363), channel_id=1, source_target_pairs={{0,1},{1,2},{2,3},{3,4},{4,5},{5,6},{6,7},{7,8},{8,9},{9,10},{10,1... | collective-permute-start | bytes 196616 | tf_op jit(solution)/shard_map/while/body/eval_jaxpr/ppermute | solution.py:10
  44.7 10.1 %collective-permute-start = (s32[256]{0:T(256)S(1)}, s32[256]{0:T(256)S(1)}, u32[]{:S(2)}, u32[]{:S(2)}) collective-permute-start(s32[256]{0:T(256)S(1)} %get-tuple-element.364), channel_id=1, source_target_pairs={{0,1},{1,2},{2,3},{3,4},{4,5},{5,6},{6,7},{7,8},{8,9},{9,10},{10,1... | collective-permute-start | bytes 3080 | tf_op jit(solution)/shard_map/while/body/eval_jaxpr/ppermute | solution.py:10
  49.0 6.0 %collective-permute-start.1 = (bf16[256,128]{1,0:T(8,128)(2,1)S(1)}, bf16[256,128]{1,0:T(8,128)(2,1)S(1)}, u32[]{:S(2)}, u32[]{:S(2)}) collective-permute-start(bf16[256,128]{1,0:T(8,128)(2,1)S(1)} %get-tuple-element.362), channel_id=1, source_target_pairs={{0,1},{1,2},{2,3},{3,4},{4,5},{5,6},{6,7},{7,8},{8,9},{9,10},{10,1... | collective-permute-start | bytes 196616 | tf_op jit(solution)/shard_map/while/body/eval_jaxpr/ppermute | solution.py:10
  50.9 5.2 %collective-permute-start.2 = (bf16[256,128]{1,0:T(8,128)(2,1)S(1)}, bf16[256,128]{1,0:T(8,128)(2,1)S(1)}, u32[]{:S(2)}, u32[]{:S(2)}) collective-permute-start(bf16[256,128]{1,0:T(8,128)(2,1)S(1)} %get-tuple-element.363), channel_id=1, source_target_pairs={{0,1},{1,2},{2,3},{3,4},{4,5},{5,6},{6,7},{7,8},{8,9},{9,10},{10,1... | collective-permute-start | bytes 196616 | tf_op jit(solution)/shard_map/while/body/eval_jaxpr/ppermute | solution.py:10
  181.4 32.3 %copy-start.2 = (f32[2]{0:T(128)}, f32[2]{0:T(128)S(1)}, u32[]{:S(2)}) copy-start(f32[2]{0:T(128)S(1)} %psum.14) | copy-start | bytes 28
where the time goes:
time: 219 us; the launch traced here: 215 us
  blocking collectives  150 us (68%)
  starting transfers between devices  37.3 us (17%)
  matrix products  7.21 us (3%)
  other arithmetic  6.55 us (3%)
  local copies, waits for them, and re-layouts  5.24 us (2%)
  waiting for transfers between devices  3.95 us (2%)
  between operations  3.93 us (2%)
    psum x1, blocking collectives, per_device(): span_scores = lax.psum(partial_value, ('phase', 'ctx'))  122 us
    ppermute x12, starting transfers between devices, passed_along(): return lax.ppermute(array, axis, pairs)  37.3 us
    psum x1, blocking collectives, per_device(): pair_loss = lax.psum(loss_term, 'dp') / lax.axis_size('dp')  28.3 us
    dot_general x5, matrix products, attend_piece(): jnp.einsum('hij,jd->hid', prob.astype(jnp.bfloat16), vpiece, preferred_el...  4.9 us
  transfers between devices with their start and end apart: 12, of which 6 were waited for; matrix products, arithmetic and copies ran while one was open for 2% of the time, Pallas kernels for 0%

commit v1 on v0

v1 whole, which is shorter than its diff:
```python
import jax
import jax.numpy as jnp
from jax import lax
from jax.sharding import PartitionSpec as P

MAX_SEGMENT = 1024


def per_device(queries, keys, values, segment_ids, span_ids, readout):
    tok = queries.shape[1]
    head_dim = keys.shape[2]
    heads = queries.shape[2] // head_dim
    n_ctx = lax.axis_size("ctx")
    back = min((MAX_SEGMENT - 1 + tok - 1) // tok, n_ctx - 1)
    here = lax.axis_index("ctx")
    qseg = segment_ids[0]
    qpos = here * tok + jnp.arange(tok)

    kv = jnp.concatenate([keys[0], values[0]], axis=1)
    segrow = jnp.broadcast_to(qseg.astype(jnp.bfloat16)[None, :], (16, tok))
    segrow = jnp.pad(segrow, ((0, 0), (0, 2 * head_dim - tok))) if tok < 2 * head_dim else segrow[:, : 2 * head_dim]
    packed = jnp.concatenate([kv, segrow], axis=0)
    pieces = []
    for d in range(back, 0, -1):
        pairs = [(i, i + d) for i in range(n_ctx - d)]
        pieces.append(lax.ppermute(packed, "ctx", pairs))
    pieces.append(packed)
    kall = jnp.concatenate([p[:tok, :head_dim] for p in pieces], axis=0)
    vall = jnp.concatenate([p[:tok, head_dim:] for p in pieces], axis=0)
    sall = jnp.concatenate([p[tok, :tok] for p in pieces], axis=0).astype(jnp.float32)
    kpos = (here - back) * tok + jnp.arange((back + 1) * tok)

    allow = (
        (kpos[None, :] <= qpos[:, None])
        & (kpos[None, :] >= 0)
        & (sall[None, :] == qseg.astype(jnp.float32)[:, None])
    )
    q3 = queries[0].reshape(tok, heads, head_dim)
    sc = jnp.einsum("ihd,jd->ihj", q3, kall, preferred_element_type=jnp.float32)
    sc = jnp.where(allow[:, None, :], sc / jnp.sqrt(jnp.float32(head_dim)), jnp.float32(-1e30))
    top = jnp.max(sc, axis=-1, keepdims=True)
    prob = jnp.where(allow[:, None, :], jnp.exp(sc - top), 0.0)
    total = jnp.sum(prob, axis=-1)
    acc = jnp.einsum(
        "ihj,jd->ihd", prob.astype(jnp.bfloat16), vall, preferred_element_type=jnp.float32
    )
    flat = (acc / total[:, :, None]).reshape(tok, heads * head_dim)
    attended = flat.astype(jnp.bfloat16)[None]
    score = jnp.sum(flat * readout[None, :], axis=1)
    spans = span_ids[0]
    partial_value = (
        jnp.stack(
            [jnp.sum(jnp.where(spans == 1, score, 0.0)), jnp.sum(jnp.where(spans == 2, score, 0.0))]
        )
        / 64.0
    )
    span_scores = lax.psum(lax.all_gather(partial_value, "ctx").sum(0), "phase")
    every = lax.all_gather(span_scores, "dp")
    pair_loss = jnp.mean(jax.nn.softplus(-(every[:, 0] - every[:, 1])))
    return (attended, span_scores[None], pair_loss)


def solution(mesh):
    in_specs = (
        P("dp", "ctx", "phase"),
        P("dp", "ctx", "phase"),
        P("dp", "ctx", "phase"),
        P("dp", "ctx"),
        P("dp", "ctx"),
        P("phase"),
    )
    out_specs = (P("dp", "ctx", "phase"), P("dp", None), P())
    return jax.shard_map(
        per_device, mesh=mesh, in_specs=in_specs, out_specs=out_specs, check_vma=False
    )
```

time: 219 us -> 99.9 us (0.46)
  the two profiles are of different devices: /device:TPU:1 before, /device:TPU:24 now
where the time goes in v1:
time: 99.9 us; the launch traced here: 99.4 us
  blocking collectives  57.7 us (58%)
  starting transfers between devices  11.5 us (12%)
  matrix products  10.3 us (10%)
  other arithmetic  6.68 us (7%)
  waiting for transfers between devices  6.55 us (7%)
  local copies, waits for them, and re-layouts  4.23 us (4%)
  between operations  2.56 us (3%)
    all_gather x1, blocking collectives, per_device(): every = lax.all_gather(span_scores, 'dp')  32.3 us
    all_gather x1, blocking collectives, per_device(): span_scores = lax.psum(lax.all_gather(partial_value, 'ctx').sum(0), 'phase')  14.9 us
    ppermute x4, starting transfers between devices, per_device(): pieces.append(lax.ppermute(packed, 'ctx', pairs))  11.5 us
    psum x1, blocking collectives, per_device(): span_scores = lax.psum(lax.all_gather(partial_value, 'ctx').sum(0), 'phase')  10.5 us
    sub x1, matrix products, per_device(): prob = jnp.where(allow[:, None, :], jnp.exp(sc - top), 0.0)  6.77 us
    ppermute x4, waiting for transfers between devices, per_device(): pieces.append(lax.ppermute(packed, 'ctx', pairs))  6.55 us
    dot_general x1, matrix products, per_device(): jnp.einsum('ihj,jd->ihd', prob.astype(jnp.bfloat16), vall, preferred_elem...  3.51 us
    unnamed x14, local copies, waits for them, and re-layouts  3.15 us
  transfers between devices with their start and end apart: 4, of which 3 were waited for; matrix products, arithmetic and copies ran while one was open for 3% of the time, Pallas kernels for 0%

profile of v1, /device:TPU:24, one launch (start us, length us, event | category | flops | bytes accessed | tf_op | source)
XLA Modules:
  0.0 99.4 jit_solution(4740379195871803648)
XLA Ops:
  0.6 0.7 convert_reduce_fusion
  1.3 0.9 pad_maximum_fusion
  2.2 4.8 %collective-permute-start = (bf16[272,256]{1,0:T(8,128)(2,1)S(1)}, bf16[272,256]{1,0:T(8,128)(2,1)S(1)}, u32[]{:S(2)}, u32[]{:S(2)}) collective-permute-start(bf16[272,256]{1,0:T(8,128)(2,1)S(1)} %pad_maximum_fusion), channel_id=1, source_target_pairs={{0,4},{1,5},{2,6},{3,7},{4,8},{5,9},{6,10},{7,11},{8,12},{9,13},{1... | collective-permute-start | bytes 417800 | tf_op jit(solution)/shard_map/ppermute | solution.py:26
  7.0 1.9 %collective-permute-start.1 = (bf16[272,256]{1,0:T(8,128)(2,1)S(1)}, bf16[272,256]{1,0:T(8,128)(2,1)S(1)}, u32[]{:S(2)}, u32[]{:S(2)}) collective-permute-start(bf16[272,256]{1,0:T(8,128)(2,1)S(1)} %pad_maximum_fusion), channel_id=1, source_target_pairs={{0,3},{1,4},{2,5},{3,6},{4,7},{5,8},{6,9},{7,10},{8,11},{9,12},{10... | collective-permute-start | bytes 417800 | tf_op jit(solution)/shard_map/ppermute | solution.py:26
  9.0 2.6 %collective-permute-start.2 = (bf16[272,256]{1,0:T(8,128)(2,1)S(1)}, bf16[272,256]{1,0:T(8,128)(2,1)S(1)}, u32[]{:S(2)}, u32[]{:S(2)}) collective-permute-start(bf16[272,256]{1,0:T(8,128)(2,1)S(1)} %pad_maximum_fusion), channel_id=1, source_target_pairs={{0,2},{1,3},{2,4},{3,5},{4,6},{5,7},{6,8},{7,9},{8,10},{9,11},{10,... | collective-permute-start | bytes 417800 | tf_op jit(solution)/shard_map/ppermute | solution.py:26
  11.6 2.1 %collective-permute-start.3 = (bf16[272,256]{1,0:T(8,128)(2,1)S(1)}, bf16[272,256]{1,0:T(8,128)(2,1)S(1)}, u32[]{:S(2)}, u32[]{:S(2)}) collective-permute-start(bf16[272,256]{1,0:T(8,128)(2,1)S(1)} %pad_maximum_fusion), channel_id=1, source_target_pairs={{0,1},{1,2},{2,3},{3,4},{4,5},{5,6},{6,7},{7,8},{8,9},{9,10},{10,1... | collective-permute-start | bytes 417800 | tf_op jit(solution)/shard_map/ppermute | solution.py:26
  13.7 0.7 compare_reduce_fusion.1
  14.5 0.7 convert_element_type.39
  15.1 1.1 %copy.22 = bf16[32,8,8,128]{3,2,1,0:T(8,128)(2,1)S(1)} copy(bf16[32,8,8,128]{3,1,2,0:T(8,128)(2,1)} %bitcast.54) | data formatting | bytes 1048576
  16.3 0.0 collective-permute-done
  16.3 2.5 %collective-permute-done.1 = bf16[272,256]{1,0:T(8,128)(2,1)S(1)} collective-permute-done((bf16[272,256]{1,0:T(8,128)(2,1)S(1)}, bf16[272,256]{1,0:T(8,128)(2,1)S(1)}, u32[]{:S(2)}, u32[]{:S(2)}) %collective-permute-start.1) | collective-permute-done | bytes 139296 | tf_op jit(solution)/shard_map/ppermute | solution.py:26
  18.8 0.2 dynamic-update-slice.10
  19.1 0.2 dynamic-update-slice.11
  19.3 3.1 %collective-permute-done.2 = bf16[272,256]{1,0:T(8,128)(2,1)S(1)} collective-permute-done((bf16[272,256]{1,0:T(8,128)(2,1)S(1)}, bf16[272,256]{1,0:T(8,128)(2,1)S(1)}, u32[]{:S(2)}, u32[]{:S(2)}) %collective-permute-start.2) | collective-permute-done | bytes 139296 | tf_op jit(solution)/shard_map/ppermute | solution.py:26
  22.4 0.2 dynamic-update-slice.12
  22.6 1.0 collective-permute-done.3
  23.6 0.2 dynamic-update-slice.13
  24.0 0.9 constant_dynamic-update-slice_fusion
  24.9 1.1 %compare_and_fusion = pred[256,1280]{0,1:T(8,128)(4,1)S(1)} fusion(f32[256]{0:T(256)S(1)} %bitcast.59, s32[256]{0:T(256)S(1)} %iota_add_fusion.1, f32[1280]{0:T(1024)S(1)} %convert_element_type.38, s32[1280]{0:T(1024)S(1)} %iota_add_fusion, pred[1280]{0:T(1024)(128)(4,1)S(1)} %broadcast_compare_fusion), kind=kLoop, calls=%fused_computation.11 | loop fusion | flops 1310720 | bytes 341248 | tf_op jit(solution)/shard_map/and | solution.py:34
  25.9 0.0 copy-start.1
  25.9 6.8 %fusion.30 = (f32[256,8]{0,1:T(8,128)S(1)}, bf16[256,8,1280]{0,2,1:T(8,128)(2,1)}) fusion(pred[256,1280]{0,1:T(8,128)(4,1)S(1)} %compare_and_fusion, bf16[256,8,128]{2,1,0:T(8,128)(2,1)S(1)} %bitcast.55, bf16[1280,128]{1,0:T(8,128)(2,1)S(1)} %get-tuple-element.26), kind=kOutput, calls=%fused_computation.55 | convolution fusion | flops 686818560 | bytes 6430720 | tf_op jit(solution)/shard_map/sub | solution.py:42
  32.7 0.0 copy-done.1
  32.7 3.5 %multiply_reduce_fusion = (f32[256]{0:T(256)S(1)}, bf16[256,8,128]{0,2,1:T(8,128)(2,1)S(1)}) fusion(f32[8,128]{1,0:T(8,128)S(1)} %bitcast.63, f32[256,8]{0,1:T(8,128)S(1)} %get-tuple-element.23, bf16[1280,128]{1,0:T(8,128)(2,1)S(1)} %get-tuple-element.27, bf16[256,8,1280]{0,2,1:T(8,128)(2,1)} %get-tuple-element.24), kind=kOutput, calls=%fused_computation.12 | convolution fusion | flops 672136960 | bytes 6108160 | tf_op jit(solution)/shard_map/ihj,jd->ihd/dot_general | solution.py:44
  36.2 0.6 select_reduce_fusion.1
  36.8 1.4 %fusion.23 = f32[1,1,2]{2,1,0:T(1,128)S(1)} fusion(f32[1,1]{1,0:T(1,128)} %bitcast.9, f32[1,1]{1,0:T(1,128)} %bitcast.8), kind=kLoop, calls=%fused_computation.46 | loop fusion | flops 4 | bytes 16
  38.2 14.9 %all-gather = f32[16,1,2]{2,1,0:T(1,128)S(1)} all-gather(f32[1,1,2]{2,1,0:T(1,128)S(1)} %fusion.23), channel_id=1, replica_groups=mesh['dp'=12,'phase'=4,'ctx'=16] {'ctx'}, dimensions={0}, use_global_device_ids=true | all-gather | bytes 136 | tf_op jit(solution)/shard_map/all_gather | solution.py:57
  53.1 10.5 %psum.7 = f32[1,2]{1,0:T(1,128)S(1)} all-reduce(f32[1,2]{1,0:T(1,128)S(1)} %bitcast.61), channel_id=1, replica_groups=mesh['dp'=12,'phase'=4,'ctx'=16] {'phase'}, use_global_device_ids=true, to_apply=%region_6.7 | all-reduce | flops 2 | bytes 16 | tf_op jit(solution)/shard_map/psum | solution.py:57
  63.7 32.3 %all-gather.1 = f32[12,1,2]{2,1,0:T(1,128)S(1)} all-gather(f32[1,1,2]{2,1,0:T(1,128)S(1)} %bitcast.62), channel_id=1, replica_groups=mesh['dp'=12,'phase'=4,'ctx'=16] {'dp'}, dimensions={0}, use_global_device_ids=true | all-gather | bytes 104 | tf_op jit(solution)/shard_map/all_gather | solution.py:58
  95.9 0.1 copy.17
  96.0 0.6 fusion.22
  96.7 1.0 %copy.18 = bf16[1,256,1024]{2,1,0:T(8,128)(2,1)} copy(bf16[1,256,1024]{1,2,0:T(8,128)(2,1)S(1)} %bitcast.56) | data formatting | bytes 1048576
  98.3 0.0 copy-done
  (17 shorter events, 0.2 us)
Async XLA Ops:
  2.2 14.1 %collective-permute-start = (bf16[272,256]{1,0:T(8,128)(2,1)S(1)}, bf16[272,256]{1,0:T(8,128)(2,1)S(1)}, u32[]{:S(2)}, u32[]{:S(2)}) collective-permute-start(bf16[272,256]{1,0:T(8,128)(2,1)S(1)} %pad_maximum_fusion), channel_id=1, source_target_pairs={{0,4},{1,5},{2,6},{3,7},{4,8},{5,9},{6,10},{7,11},{8,12},{9,13},{1... | collective-permute-start | bytes 417800 | tf_op jit(solution)/shard_map/ppermute | solution.py:26
  7.0 11.8 %collective-permute-start.1 = (bf16[272,256]{1,0:T(8,128)(2,1)S(1)}, bf16[272,256]{1,0:T(8,128)(2,1)S(1)}, u32[]{:S(2)}, u32[]{:S(2)}) collective-permute-start(bf16[272,256]{1,0:T(8,128)(2,1)S(1)} %pad_maximum_fusion), channel_id=1, source_target_pairs={{0,3},{1,4},{2,5},{3,6},{4,7},{5,8},{6,9},{7,10},{8,11},{9,12},{10... | collective-permute-start | bytes 417800 | tf_op jit(solution)/shard_map/ppermute | solution.py:26
  9.0 13.4 %collective-permute-start.2 = (bf16[272,256]{1,0:T(8,128)(2,1)S(1)}, bf16[272,256]{1,0:T(8,128)(2,1)S(1)}, u32[]{:S(2)}, u32[]{:S(2)}) collective-permute-start(bf16[272,256]{1,0:T(8,128)(2,1)S(1)} %pad_maximum_fusion), channel_id=1, source_target_pairs={{0,2},{1,3},{2,4},{3,5},{4,6},{5,7},{6,8},{7,9},{8,10},{9,11},{10,... | collective-permute-start | bytes 417800 | tf_op jit(solution)/shard_map/ppermute | solution.py:26
  11.6 12.0 %collective-permute-start.3 = (bf16[272,256]{1,0:T(8,128)(2,1)S(1)}, bf16[272,256]{1,0:T(8,128)(2,1)S(1)}, u32[]{:S(2)}, u32[]{:S(2)}) collective-permute-start(bf16[272,256]{1,0:T(8,128)(2,1)S(1)} %pad_maximum_fusion), channel_id=1, source_target_pairs={{0,1},{1,2},{2,3},{3,4},{4,5},{5,6},{6,7},{7,8},{8,9},{9,10},{10,1... | collective-permute-start | bytes 417800 | tf_op jit(solution)/shard_map/ppermute | solution.py:26
  25.9 6.8 %copy-start.1 = (f32[1024]{0:T(1024)S(1)}, f32[1024]{0:T(1024)}, u32[]{:S(2)}) copy-start(f32[1024]{0:T(1024)} %param.11) | copy-start | bytes 12292
  63.7 34.7 %copy-start = (f32[1,2]{1,0:T(1,128)}, f32[1,2]{1,0:T(1,128)S(1)}, u32[]{:S(2)}) copy-start(f32[1,2]{1,0:T(1,128)S(1)} %psum.7) | copy-start | bytes 28

commit v2 on v1

v2 whole, which is shorter than its diff:
```python
import functools
import jax
import jax.numpy as jnp
from jax import lax
from jax.experimental import pallas as pl
from jax.experimental.pallas import tpu as pltpu
from jax.sharding import PartitionSpec as P

MAX_SEGMENT = 1024


def attend_kernel(q_ref, k_ref, v_ref, qpos_ref, qseg_ref, kpos_ref, kseg_ref, r_ref, o_ref, s_ref):
    h = pl.program_id(0)
    allow = (
        (kpos_ref[...] <= qpos_ref[...])
        & (kpos_ref[...] >= 0)
        & (kseg_ref[...] == qseg_ref[...])
    )
    scale = 1.0 / jnp.sqrt(jnp.float32(q_ref.shape[1]))
    sc = lax.dot_general(
        q_ref[...], k_ref[...], (((1,), (1,)), ((), ())), preferred_element_type=jnp.float32
    )
    sc = jnp.where(allow, sc * scale, jnp.float32(-1e30))
    top = jnp.max(sc, axis=1, keepdims=True)
    prob = jnp.where(allow, jnp.exp(sc - top), 0.0)
    total = jnp.sum(prob, axis=1, keepdims=True)
    acc = jnp.dot(prob.astype(jnp.bfloat16), v_ref[...], preferred_element_type=jnp.float32)
    full = acc / total
    o_ref[...] = full.astype(o_ref.dtype)
    part = jnp.sum(full * r_ref[...], axis=1, keepdims=True)

    @pl.when(h == 0)
    def _():
        s_ref[...] = part

    @pl.when(h > 0)
    def _():
        s_ref[...] += part


def attend(q, kall, vall, qpos, qseg, kpos, kseg, readout, interpret=False):
    tok, width = q.shape
    nk, hd = kall.shape
    heads = width // hd
    return pl.pallas_call(
        attend_kernel,
        grid=(heads,),
        in_specs=[
            pl.BlockSpec((tok, hd), lambda h: (0, h)),
            pl.BlockSpec((nk, hd), lambda h: (0, 0)),
            pl.BlockSpec((nk, hd), lambda h: (0, 0)),
            pl.BlockSpec((tok, 1), lambda h: (0, 0)),
            pl.BlockSpec((tok, 1), lambda h: (0, 0)),
            pl.BlockSpec((1, nk), lambda h: (0, 0)),
            pl.BlockSpec((1, nk), lambda h: (0, 0)),
            pl.BlockSpec((1, hd), lambda h: (0, h)),
        ],
        out_specs=[
            pl.BlockSpec((tok, hd), lambda h: (0, h)),
            pl.BlockSpec((tok, 1), lambda h: (0, 0)),
        ],
        out_shape=[
            jax.ShapeDtypeStruct((tok, width), jnp.bfloat16),
            jax.ShapeDtypeStruct((tok, 1), jnp.float32),
        ],
        compiler_params=pltpu.CompilerParams(dimension_semantics=("arbitrary",)),
        interpret=interpret,
    )(q, kall, vall, qpos, qseg, kpos, kseg, readout)


def per_device(queries, keys, values, segment_ids, span_ids, readout):
    tok = queries.shape[1]
    head_dim = keys.shape[2]
    n_ctx = lax.axis_size("ctx")
    back = min((MAX_SEGMENT - 1 + tok - 1) // tok, n_ctx - 1)
    here = lax.axis_index("ctx")
    qseg = segment_ids[0]
    qpos = here * tok + jnp.arange(tok)

    kv = jnp.concatenate([keys[0], values[0]], axis=1)
    segrow = jnp.broadcast_to(qseg.astype(jnp.bfloat16)[None, :], (16, tok))
    segrow = jnp.pad(segrow, ((0, 0), (0, 2 * head_dim - tok))) if tok < 2 * head_dim else segrow[:, : 2 * head_dim]
    packed = jnp.concatenate([kv, segrow], axis=0)
    pieces = []
    for d in range(back, 0, -1):
        pairs = [(i, i + d) for i in range(n_ctx - d)]
        pieces.append(lax.ppermute(packed, "ctx", pairs))
    pieces.append(packed)
    kall = jnp.concatenate([p[:tok, :head_dim] for p in pieces], axis=0)
    vall = jnp.concatenate([p[:tok, head_dim:] for p in pieces], axis=0)
    sall = jnp.concatenate([p[tok, :tok] for p in pieces], axis=0).astype(jnp.float32)
    kpos = (here - back) * tok + jnp.arange((back + 1) * tok, dtype=jnp.int32)

    attended, score = attend(
        queries[0], kall, vall,
        qpos.astype(jnp.int32)[:, None], qseg.astype(jnp.float32)[:, None],
        kpos[None, :], sall[None, :], readout[None, :],
    )
    score = score[:, 0]
    spans = span_ids[0]
    partial_value = (
        jnp.stack(
            [jnp.sum(jnp.where(spans == 1, score, 0.0)), jnp.sum(jnp.where(spans == 2, score, 0.0))]
        )
        / 64.0
    )
    span_scores = lax.psum(lax.all_gather(partial_value, "ctx").sum(0), "phase")
    every = lax.all_gather(span_scores, "dp")
    pair_loss = jnp.mean(jax.nn.softplus(-(every[:, 0] - every[:, 1])))
    return (attended[None], span_scores[None], pair_loss)


def solution(mesh):
    in_specs = (
        P("dp", "ctx", "phase"),
        P("dp", "ctx", "phase"),
        P("dp", "ctx", "phase"),
        P("dp", "ctx"),
        P("dp", "ctx"),
        P("phase"),
    )
    out_specs = (P("dp", "ctx", "phase"), P("dp", None), P())
    return jax.shard_map(
        per_device, mesh=mesh, in_specs=in_specs, out_specs=out_specs, check_vma=False
    )
```

time: 99.9 us -> 104 us (1.041)
  Pallas kernels: 0 us -> 13.4 us
  matrix products: 10.3 us -> 0 us
  waiting for transfers between devices: 6.55 us -> 7.68 us
    pallas_call x0 -> x1, Pallas kernels: none -> 13.4 us  [attend(): pl.pallas_call(attend_kernel, grid=(heads,), in_specs=[pl.BlockSpec((tok,...]
    sub x1 -> x0, matrix products: 6.77 us -> none  [per_device(): prob = jnp.where(allow[:, None, :], jnp.exp(sc - top), 0.0)]
    dot_general x1 -> x0, matrix products: 3.51 us -> none  [per_device(): jnp.einsum('ihj,jd->ihd', prob.astype(jnp.bfloat16), vall, preferred_elem...]
    ppermute x4, waiting for transfers between devices: 6.55 us -> 7.68 us  [per_device(): pieces.append(lax.ppermute(packed, 'ctx', pairs))]
    and x1 -> x0, other arithmetic: 1.05 us -> none  [per_device(): (kpos[None, :] <= qpos[:, None]) & (kpos[None, :] >= 0)]
    unnamed x14 -> x22, local copies, waits for them, and re-layouts: 3.15 us -> 2.36 us
  transfers between devices with their start and end apart: 4 -> 4, of which waited for: 3 -> 3; matrix products, arithmetic and copies ran while one was open for 3% -> 2% of each run, Pallas kernels for 0% -> 0%
where the time goes in v2:
time: 104 us; the launch traced here: 103 us
  blocking collectives  57.7 us (55%)
  Pallas kernels  13.4 us (13%)
  starting transfers between devices  11.5 us (11%)
  waiting for transfers between devices  7.68 us (7%)
  other arithmetic  7.11 us (7%)
  local copies, waits for them, and re-layouts  3.27 us (3%)
  between operations  2.56 us (2%)
    all_gather x1, blocking collectives, per_device(): every = lax.all_gather(span_scores, 'dp')  32.3 us
    all_gather x1, blocking collectives, per_device(): span_scores = lax.psum(lax.all_gather(partial_value, 'ctx').sum(0), 'phase')  14.9 us
    pallas_call x1, Pallas kernels, attend(): pl.pallas_call(attend_kernel, grid=(heads,), in_specs=[pl.BlockSpec((tok,...  13.4 us
    ppermute x4, starting transfers between devices, per_device(): pieces.append(lax.ppermute(packed, 'ctx', pairs))  11.5 us
    psum x1, blocking collectives, per_device(): span_scores = lax.psum(lax.all_gather(partial_value, 'ctx').sum(0), 'phase')  10.5 us
    ppermute x4, waiting for transfers between devices, per_device(): pieces.append(lax.ppermute(packed, 'ctx', pairs))  7.68 us
    unnamed x22, local copies, waits for them, and re-layouts  2.36 us
  transfers between devices with their start and end apart: 4, of which 3 were waited for; matrix products, arithmetic and copies ran while one was open for 2% of the time, Pallas kernels for 0%

profile of v2, /device:TPU:24, one launch (start us, length us, event | category | flops | bytes accessed | tf_op | source)
XLA Modules:
  0.0 103.2 jit_solution(12881943714983660570)
XLA Ops:
  0.6 0.7 convert_reduce_fusion
  1.3 0.9 pad_maximum_fusion
  2.2 0.0 copy-start.4
  2.2 4.8 %collective-permute-start = (bf16[272,256]{1,0:T(8,128)(2,1)S(1)}, bf16[272,256]{1,0:T(8,128)(2,1)S(1)}, u32[]{:S(2)}, u32[]{:S(2)}) collective-permute-start(bf16[272,256]{1,0:T(8,128)(2,1)S(1)} %pad_maximum_fusion), channel_id=1, source_target_pairs={{0,4},{1,5},{2,6},{3,7},{4,8},{5,9},{6,10},{7,11},{8,12},{9,13},{1... | collective-permute-start | bytes 417800 | tf_op jit(solution)/shard_map/ppermute | solution.py:87
  7.1 1.9 %collective-permute-start.1 = (bf16[272,256]{1,0:T(8,128)(2,1)S(1)}, bf16[272,256]{1,0:T(8,128)(2,1)S(1)}, u32[]{:S(2)}, u32[]{:S(2)}) collective-permute-start(bf16[272,256]{1,0:T(8,128)(2,1)S(1)} %pad_maximum_fusion), channel_id=1, source_target_pairs={{0,3},{1,4},{2,5},{3,6},{4,7},{5,8},{6,9},{7,10},{8,11},{9,12},{10... | collective-permute-start | bytes 417800 | tf_op jit(solution)/shard_map/ppermute | solution.py:87
  9.0 2.6 %collective-permute-start.2 = (bf16[272,256]{1,0:T(8,128)(2,1)S(1)}, bf16[272,256]{1,0:T(8,128)(2,1)S(1)}, u32[]{:S(2)}, u32[]{:S(2)}) collective-permute-start(bf16[272,256]{1,0:T(8,128)(2,1)S(1)} %pad_maximum_fusion), channel_id=1, source_target_pairs={{0,2},{1,3},{2,4},{3,5},{4,6},{5,7},{6,8},{7,9},{8,10},{9,11},{10,... | collective-permute-start | bytes 417800 | tf_op jit(solution)/shard_map/ppermute | solution.py:87
  11.6 2.1 %collective-permute-start.3 = (bf16[272,256]{1,0:T(8,128)(2,1)S(1)}, bf16[272,256]{1,0:T(8,128)(2,1)S(1)}, u32[]{:S(2)}, u32[]{:S(2)}) collective-permute-start(bf16[272,256]{1,0:T(8,128)(2,1)S(1)} %pad_maximum_fusion), channel_id=1, source_target_pairs={{0,1},{1,2},{2,3},{3,4},{4,5},{5,6},{6,7},{7,8},{8,9},{9,10},{10,1... | collective-permute-start | bytes 417800 | tf_op jit(solution)/shard_map/ppermute | solution.py:87
  13.8 0.0 copy-start.5
  13.8 0.6 iota_add_fusion.1.kpos_ref
  14.4 0.1 copy-done.5
  14.5 0.8 copy.12.qseg_ref
  15.3 0.6 iota_add_fusion.qpos_ref
  15.9 2.9 %collective-permute-done.1 = bf16[272,256]{1,0:T(8,128)(2,1)S(1)} collective-permute-done((bf16[272,256]{1,0:T(8,128)(2,1)S(1)}, bf16[272,256]{1,0:T(8,128)(2,1)S(1)}, u32[]{:S(2)}, u32[]{:S(2)}) %collective-permute-start.1) | collective-permute-done | bytes 139296 | tf_op jit(solution)/shard_map/ppermute | solution.py:87
  18.8 3.5 %collective-permute-done.2 = bf16[272,256]{1,0:T(8,128)(2,1)S(1)} collective-permute-done((bf16[272,256]{1,0:T(8,128)(2,1)S(1)}, bf16[272,256]{1,0:T(8,128)(2,1)S(1)}, u32[]{:S(2)}, u32[]{:S(2)}) %collective-permute-start.2) | collective-permute-done | bytes 139296 | tf_op jit(solution)/shard_map/ppermute | solution.py:87
  22.4 1.2 %collective-permute-done.3 = bf16[272,256]{1,0:T(8,128)(2,1)S(1)} collective-permute-done((bf16[272,256]{1,0:T(8,128)(2,1)S(1)}, bf16[272,256]{1,0:T(8,128)(2,1)S(1)}, u32[]{:S(2)}, u32[]{:S(2)}) %collective-permute-start.3) | collective-permute-done | bytes 139296 | tf_op jit(solution)/shard_map/ppermute | solution.py:87
  23.6 0.6 convert_element_type.30.kseg_ref
  24.3 0.0 copy-start.2
  24.3 0.0 copy-start.3
  24.4 0.8 copy-done.2
  25.1 0.0 copy-done.3
  25.2 0.7 copy-done
  25.9 0.1 copy-done.1
  26.0 13.4 %shard_map.85 = (bf16[256,1024]{1,0:T(8,128)(2,1)}, f32[256,1]{1,0:T(8,128)}) custom-call(bf16[256,1024]{1,0:T(8,128)(2,1)} %bitcast.32, bf16[1280,128]{1,0:T(8,128)(2,1)} %copy-done.1, bf16[1280,128]{1,0:T(8,128)(2,1)} %copy-done, s32[256,1]{1,0:T(8,128)} %iota_add_fusion.qpos_ref, f32[256,1]{1,0:T(8,128)} %copy.12.qseg_ref, ...), custom_call_target="tpu_custom_call" | custom-call | tf_op jit(solution)/shard_map/pallas_call | solution.py:45
  39.4 1.0 reduce.3
  40.5 0.6 select_reduce_fusion.1
  41.1 1.4 %fusion.1 = f32[1,1,2]{2,1,0:T(1,128)S(1)} fusion(f32[1,1]{1,0:T(1,128)} %bitcast.7, f32[1,1]{1,0:T(1,128)} %bitcast.6), kind=kLoop, calls=%fused_computation.27 | loop fusion | flops 4 | bytes 16
  42.4 14.9 %all-gather = f32[16,1,2]{2,1,0:T(1,128)S(1)} all-gather(f32[1,1,2]{2,1,0:T(1,128)S(1)} %fusion.1), channel_id=1, replica_groups=mesh['dp'=12,'phase'=4,'ctx'=16] {'ctx'}, dimensions={0}, use_global_device_ids=true | all-gather | bytes 136 | tf_op jit(solution)/shard_map/all_gather | solution.py:107
  57.4 10.5 %psum.7 = f32[1,2]{1,0:T(1,128)S(1)} all-reduce(f32[1,2]{1,0:T(1,128)S(1)} %bitcast.37), channel_id=1, replica_groups=mesh['dp'=12,'phase'=4,'ctx'=16] {'phase'}, use_global_device_ids=true, to_apply=%region_3.4 | all-reduce | flops 2 | bytes 16 | tf_op jit(solution)/shard_map/psum | solution.py:107
  67.9 0.5 copy-done.6
  68.4 32.3 %all-gather.1 = f32[12,1,2]{2,1,0:T(1,128)S(1)} all-gather(f32[1,1,2]{2,1,0:T(1,128)S(1)} %bitcast.38), channel_id=1, replica_groups=mesh['dp'=12,'phase'=4,'ctx'=16] {'dp'}, dimensions={0}, use_global_device_ids=true | all-gather | bytes 104 | tf_op jit(solution)/shard_map/all_gather | solution.py:108
  100.7 0.1 copy.13
  100.8 0.6 fusion
  (19 shorter events, 0.2 us)
Async XLA Ops:
  2.2 11.5 %copy-start.4 = (s32[1,256]{1,0:T(1,128)S(1)}, s32[1,256]{1,0:T(1,128)}, u32[]{:S(2)}) copy-start(s32[1,256]{1,0:T(1,128)} %param.9) | copy-start | bytes 3076
  2.2 13.7 %collective-permute-start = (bf16[272,256]{1,0:T(8,128)(2,1)S(1)}, bf16[272,256]{1,0:T(8,128)(2,1)S(1)}, u32[]{:S(2)}, u32[]{:S(2)}) collective-permute-start(bf16[272,256]{1,0:T(8,128)(2,1)S(1)} %pad_maximum_fusion), channel_id=1, source_target_pairs={{0,4},{1,5},{2,6},{3,7},{4,8},{5,9},{6,10},{7,11},{8,12},{9,13},{1... | collective-permute-start | bytes 417800 | tf_op jit(solution)/shard_map/ppermute | solution.py:87
  7.1 11.8 %collective-permute-start.1 = (bf16[272,256]{1,0:T(8,128)(2,1)S(1)}, bf16[272,256]{1,0:T(8,128)(2,1)S(1)}, u32[]{:S(2)}, u32[]{:S(2)}) collective-permute-start(bf16[272,256]{1,0:T(8,128)(2,1)S(1)} %pad_maximum_fusion), channel_id=1, source_target_pairs={{0,3},{1,4},{2,5},{3,6},{4,7},{5,8},{6,9},{7,10},{8,11},{9,12},{10... | collective-permute-start | bytes 417800 | tf_op jit(solution)/shard_map/ppermute | solution.py:87
  9.0 13.4 %collective-permute-start.2 = (bf16[272,256]{1,0:T(8,128)(2,1)S(1)}, bf16[272,256]{1,0:T(8,128)(2,1)S(1)}, u32[]{:S(2)}, u32[]{:S(2)}) collective-permute-start(bf16[272,256]{1,0:T(8,128)(2,1)S(1)} %pad_maximum_fusion), channel_id=1, source_target_pairs={{0,2},{1,3},{2,4},{3,5},{4,6},{5,7},{6,8},{7,9},{8,10},{9,11},{10,... | collective-permute-start | bytes 417800 | tf_op jit(solution)/shard_map/ppermute | solution.py:87
  11.6 12.0 %collective-permute-start.3 = (bf16[272,256]{1,0:T(8,128)(2,1)S(1)}, bf16[272,256]{1,0:T(8,128)(2,1)S(1)}, u32[]{:S(2)}, u32[]{:S(2)}) collective-permute-start(bf16[272,256]{1,0:T(8,128)(2,1)S(1)} %pad_maximum_fusion), channel_id=1, source_target_pairs={{0,1},{1,2},{2,3},{3,4},{4,5},{5,6},{6,7},{7,8},{8,9},{9,10},{10,1... | collective-permute-start | bytes 417800 | tf_op jit(solution)/shard_map/ppermute | solution.py:87
  13.8 0.7 copy-start.5
  24.3 0.8 copy-start.2
  24.3 0.9 copy-start.3
  25.2 0.7 copy-start
  25.2 0.8 copy-start.1
  67.9 0.5 copy-start.6

commit v3 on v1

v3 whole, which is shorter than its diff:
```python
import jax
import jax.numpy as jnp
from jax import lax
from jax.experimental import pallas as pl
from jax.experimental.pallas import tpu as pltpu
from jax.sharding import PartitionSpec as P

MAX_SEGMENT = 1024
MASKED = -1e30


def attend_kernel(here_ref, *refs):
    npieces = len(refs) - 10
    pieces = refs[:npieces]
    q_ref, qseg_ref, span_ref, r_ref, o_ref, part_ref, k_all, v_all, bias, score = refs[npieces:]
    h = pl.program_id(0)
    tok, hd = q_ref.shape

    @pl.when(h == 0)
    def _():
        here = here_ref[0]
        qpos = here * tok + lax.broadcasted_iota(jnp.int32, (tok, 1), 0)
        qseg = qseg_ref[...]
        for i, p_ref in enumerate(pieces):
            k_all[pl.ds(i * tok, tok), :] = p_ref[pl.ds(0, tok), pl.ds(0, hd)]
            v_all[pl.ds(i * tok, tok), :] = p_ref[pl.ds(0, tok), pl.ds(hd, hd)]
            kseg = p_ref[pl.ds(tok, 16), pl.ds(0, tok)].astype(jnp.float32)[0:1, :]
            kpos = (here - (npieces - 1 - i)) * tok + lax.broadcasted_iota(jnp.int32, (1, tok), 1)
            allow = (kpos <= qpos) & (kpos >= 0) & (kseg == qseg)
            bias[:, pl.ds(i * tok, tok)] = jnp.where(allow, 0.0, MASKED)
        score[...] = jnp.zeros_like(score)

    scale = 1.0 / jnp.sqrt(jnp.float32(hd))
    sc = lax.dot_general(
        q_ref[...], k_all[...], (((1,), (1,)), ((), ())), preferred_element_type=jnp.float32
    )
    sc = sc * scale + bias[...]
    top = jnp.max(sc, axis=1, keepdims=True)
    prob = jnp.exp(sc - top)
    total = jnp.sum(prob, axis=1, keepdims=True)
    acc = jnp.dot(prob.astype(jnp.bfloat16), v_all[...], preferred_element_type=jnp.float32)
    full = acc / total
    o_ref[...] = full.astype(o_ref.dtype)
    score[...] += jnp.sum(full * r_ref[...], axis=1, keepdims=True)

    @pl.when(h == pl.num_programs(0) - 1)
    def _():
        spans = span_ref[...]
        s = score[...]
        chosen = jnp.sum(jnp.where(spans == 1, s, 0.0), axis=0, keepdims=True)
        reject = jnp.sum(jnp.where(spans == 2, s, 0.0), axis=0, keepdims=True)
        part_ref[...] = jnp.concatenate([chosen, reject], axis=1) / 64.0


def attend(here, pieces, q, qseg, spans, readout, interpret=False):
    tok, width = q.shape
    hd = pieces[0].shape[1] // 2
    heads = width // hd
    n = len(pieces)
    full = lambda shape: pl.BlockSpec(shape, lambda h, here: (0, 0))
    grid_spec = pltpu.PrefetchScalarGridSpec(
        num_scalar_prefetch=1,
        grid=(heads,),
        in_specs=[full(p.shape) for p in pieces]
        + [
            pl.BlockSpec((tok, hd), lambda h, here: (0, h)),
            full((tok, 1)),
            full((tok, 1)),
            pl.BlockSpec((1, hd), lambda h, here: (0, h)),
        ],
        out_specs=[pl.BlockSpec((tok, hd), lambda h, here: (0, h)), full((1, 2))],
        scratch_shapes=[
            pltpu.VMEM((n * tok, hd), jnp.bfloat16),
            pltpu.VMEM((n * tok, hd), jnp.bfloat16),
            pltpu.VMEM((tok, n * tok), jnp.float32),
            pltpu.VMEM((tok, 1), jnp.float32),
        ],
    )
    return pl.pallas_call(
        attend_kernel,
        grid_spec=grid_spec,
        out_shape=[
            jax.ShapeDtypeStruct((tok, width), jnp.bfloat16),
            jax.ShapeDtypeStruct((1, 2), jnp.float32),
        ],
        compiler_params=pltpu.CompilerParams(dimension_semantics=("arbitrary",)),
        interpret=interpret,
    )(here, *pieces, q, qseg, spans, readout)


def per_device(queries, keys, values, segment_ids, span_ids, readout):
    tok = queries.shape[1]
    head_dim = keys.shape[2]
    n_ctx = lax.axis_size("ctx")
    back = min((MAX_SEGMENT - 1 + tok - 1) // tok, n_ctx - 1)
    here = lax.axis_index("ctx")
    qseg = segment_ids[0]

    kv = jnp.concatenate([keys[0], values[0]], axis=1)
    segrow = jnp.broadcast_to(qseg.astype(jnp.bfloat16)[None, :], (16, tok))
    segrow = jnp.pad(segrow, ((0, 0), (0, 2 * head_dim - tok))) if tok < 2 * head_dim else segrow[:, : 2 * head_dim]
    packed = jnp.concatenate([kv, segrow], axis=0)
    pieces = []
    for d in range(back, 0, -1):
        pairs = [(i, i + d) for i in range(n_ctx - d)]
        pieces.append(lax.ppermute(packed, "ctx", pairs))
    pieces.append(packed)

    attended, part = attend(
        jnp.reshape(here, (1,)).astype(jnp.int32), pieces, queries[0],
        qseg.astype(jnp.float32)[:, None], span_ids[0][:, None], readout[None, :],
    )
    span_scores = lax.psum(lax.all_gather(part[0], "ctx").sum(0), "phase")
    every = lax.all_gather(span_scores, "dp")
    pair_loss = jnp.mean(jax.nn.softplus(-(every[:, 0] - every[:, 1])))
    return (attended[None], span_scores[None], pair_loss)


def solution(mesh):
    in_specs = (
        P("dp", "ctx", "phase"),
        P("dp", "ctx", "phase"),
        P("dp", "ctx", "phase"),
        P("dp", "ctx"),
        P("dp", "ctx"),
        P("phase"),
    )
    out_specs = (P("dp", "ctx", "phase"), P("dp", None), P())
    return jax.shard_map(
        per_device, mesh=mesh, in_specs=in_specs, out_specs=out_specs, check_vma=False
    )
```

time: 99.9 us -> 97.7 us (0.978)
  the two profiles are of different devices: /device:TPU:24 before, /device:TPU:2 now
where the time goes in v3:
time: 97.7 us; the launch traced here: 97.3 us
  blocking collectives  62.5 us (64%)
  starting transfers between devices  14.7 us (15%)
  Pallas kernels  10.2 us (10%)
  local copies, waits for them, and re-layouts  4.87 us (5%)
  between operations  2.5 us (3%)
  other arithmetic  2.25 us (2%)
    all_gather x1, blocking collectives, per_device(): every = lax.all_gather(span_scores, 'dp')  32.3 us
    all_gather x1, blocking collectives, per_device(): span_scores = lax.psum(lax.all_gather(part[0], 'ctx').sum(0), 'phase')  21.6 us
    ppermute x4, starting transfers between devices, per_device(): pieces.append(lax.ppermute(packed, 'ctx', pairs))  14.7 us
    pallas_call x1, Pallas kernels, attend(): pl.pallas_call(attend_kernel, grid_spec=grid_spec, out_shape=[jax.ShapeDt...  10.2 us
    psum x1, blocking collectives, per_device(): span_scores = lax.psum(lax.all_gather(part[0], 'ctx').sum(0), 'phase')  8.62 us
    unnamed x18, local copies, waits for them, and re-layouts  3.17 us
  transfers between devices with their start and end apart: 4, of which 1 were waited for; matrix products, arithmetic and copies ran while one was open for 2% of the time, Pallas kernels for 0%

profile of v3, /device:TPU:2, one launch (start us, length us, event | category | flops | bytes accessed | tf_op | source)
XLA Modules:
  0.0 97.3 jit_solution(15527498913500025114)
XLA Ops:
  0.6 0.7 convert_reduce_fusion
  1.3 0.9 pad_maximum_fusion.refs_4_
  2.2 0.0 copy-start
  2.2 1.7 %collective-permute-start.3 = (bf16[272,256]{1,0:T(8,128)(2,1)S(1)}, bf16[272,256]{1,0:T(8,128)(2,1)S(1)}, u32[]{:S(2)}, u32[]{:S(2)}) collective-permute-start(bf16[272,256]{1,0:T(8,128)(2,1)S(1)} %pad_maximum_fusion.refs_4_), channel_id=1, source_target_pairs={{0,1},{1,2},{2,3},{3,4},{4,5},{5,6},{6,7},{7,8},{8,9},{9,10},{10,1... | collective-permute-start | bytes 417800 | tf_op jit(solution)/shard_map/ppermute | solution.py:106
  4.0 3.7 %collective-permute-start.2 = (bf16[272,256]{1,0:T(8,128)(2,1)S(1)}, bf16[272,256]{1,0:T(8,128)(2,1)S(1)}, u32[]{:S(2)}, u32[]{:S(2)}) collective-permute-start(bf16[272,256]{1,0:T(8,128)(2,1)S(1)} %pad_maximum_fusion.refs_4_), channel_id=1, source_target_pairs={{0,2},{1,3},{2,4},{3,5},{4,6},{5,7},{6,8},{7,9},{8,10},{9,11},{10,... | collective-permute-start | bytes 417800 | tf_op jit(solution)/shard_map/ppermute | solution.py:106
  7.7 4.5 %collective-permute-start.1 = (bf16[272,256]{1,0:T(8,128)(2,1)S(1)}, bf16[272,256]{1,0:T(8,128)(2,1)S(1)}, u32[]{:S(2)}, u32[]{:S(2)}) collective-permute-start(bf16[272,256]{1,0:T(8,128)(2,1)S(1)} %pad_maximum_fusion.refs_4_), channel_id=1, source_target_pairs={{0,3},{1,4},{2,5},{3,6},{4,7},{5,8},{6,9},{7,10},{8,11},{9,12},{10... | collective-permute-start | bytes 417800 | tf_op jit(solution)/shard_map/ppermute | solution.py:106
  12.2 4.8 %collective-permute-start = (bf16[272,256]{1,0:T(8,128)(2,1)S(1)}, bf16[272,256]{1,0:T(8,128)(2,1)S(1)}, u32[]{:S(2)}, u32[]{:S(2)}) collective-permute-start(bf16[272,256]{1,0:T(8,128)(2,1)S(1)} %pad_maximum_fusion.refs_4_), channel_id=1, source_target_pairs={{0,4},{1,5},{2,6},{3,7},{4,8},{5,9},{6,10},{7,11},{8,12},{9,13},{1... | collective-permute-start | bytes 417800 | tf_op jit(solution)/shard_map/ppermute | solution.py:106
  17.0 0.0 copy-start.6
  17.0 0.7 copy-done.6
  17.7 0.8 copy.13.refs_6_
  18.5 0.7 copy-done.5
  19.1 0.8 copy.14.refs_7_
  19.9 0.0 collective-permute-done.3.refs_3_
  20.0 0.0 copy-start.1
  20.0 0.0 collective-permute-done.2.refs_2_
  20.0 0.0 copy-start.2
  20.0 0.0 collective-permute-done.1.refs_1_
  20.0 0.0 copy-start.3
  20.0 0.2 collective-permute-done.refs_0_
  20.2 0.0 copy-done
  20.2 0.4 copy-done.1
  20.6 0.1 copy-done.2
  20.7 0.1 copy-done.3
  20.7 0.1 copy-done.4
  20.9 10.2 %shard_map.85 = (bf16[256,1024]{1,0:T(8,128)(2,1)}, f32[1,2]{1,0:T(1,128)}) custom-call(s32[1]{0:T(128)} %bitcast.here_ref, bf16[272,256]{1,0:T(8,128)(2,1)} %copy-done.4, bf16[272,256]{1,0:T(8,128)(2,1)} %copy-done.3, bf16[272,256]{1,0:T(8,128)(2,1)} %copy-done.2, bf16[272,256]{1,0:T(8,128)(2,1)} %copy-done.1, bf16[272,256]{1,0:T(8,128)(2,1)} %copy-done, ...), custom_call_target="tpu_custom_call" | custom-call | tf_op jit(solution)/shard_map/pallas_call | solution.py:79
  31.1 0.7 copy-done.7
  31.7 21.6 %all-gather = f32[16,1,2]{2,1,0:T(1,128)S(1)} all-gather(f32[1,1,2]{2,1,0:T(1,128)S(1)} %bitcast.35), channel_id=1, replica_groups=mesh['dp'=12,'phase'=4,'ctx'=16] {'ctx'}, dimensions={0}, use_global_device_ids=true | all-gather | bytes 136 | tf_op jit(solution)/shard_map/all_gather | solution.py:113
  53.4 8.6 %psum.7 = f32[1,2]{1,0:T(1,128)S(1)} all-reduce(f32[1,2]{1,0:T(1,128)S(1)} %bitcast.36), channel_id=1, replica_groups=mesh['dp'=12,'phase'=4,'ctx'=16] {'phase'}, use_global_device_ids=true, to_apply=%region_1.0 | all-reduce | flops 2 | bytes 16 | tf_op jit(solution)/shard_map/psum | solution.py:113
  62.0 0.5 copy-done.8
  62.5 32.3 %all-gather.1 = f32[12,1,2]{2,1,0:T(1,128)S(1)} all-gather(f32[1,1,2]{2,1,0:T(1,128)S(1)} %bitcast.37), channel_id=1, replica_groups=mesh['dp'=12,'phase'=4,'ctx'=16] {'dp'}, dimensions={0}, use_global_device_ids=true | all-gather | bytes 104 | tf_op jit(solution)/shard_map/all_gather | solution.py:114
  94.8 0.1 copy.15
  94.9 0.6 fusion
  (7 shorter events, 0.1 us)
Async XLA Ops:
  2.2 18.0 %copy-start = (bf16[272,256]{1,0:T(8,128)(2,1)}, bf16[272,256]{1,0:T(8,128)(2,1)S(1)}, u32[]{:S(2)}) copy-start(bf16[272,256]{1,0:T(8,128)(2,1)S(1)} %pad_maximum_fusion.refs_4_) | copy-start | bytes 417796
  2.2 17.7 %collective-permute-start.3 = (bf16[272,256]{1,0:T(8,128)(2,1)S(1)}, bf16[272,256]{1,0:T(8,128)(2,1)S(1)}, u32[]{:S(2)}, u32[]{:S(2)}) collective-permute-start(bf16[272,256]{1,0:T(8,128)(2,1)S(1)} %pad_maximum_fusion.refs_4_), channel_id=1, source_target_pairs={{0,1},{1,2},{2,3},{3,4},{4,5},{5,6},{6,7},{7,8},{8,9},{9,10},{10,1... | collective-permute-start | bytes 417800 | tf_op jit(solution)/shard_map/ppermute | solution.py:106
  4.0 16.0 %collective-permute-start.2 = (bf16[272,256]{1,0:T(8,128)(2,1)S(1)}, bf16[272,256]{1,0:T(8,128)(2,1)S(1)}, u32[]{:S(2)}, u32[]{:S(2)}) collective-permute-start(bf16[272,256]{1,0:T(8,128)(2,1)S(1)} %pad_maximum_fusion.refs_4_), channel_id=1, source_target_pairs={{0,2},{1,3},{2,4},{3,5},{4,6},{5,7},{6,8},{7,9},{8,10},{9,11},{10,... | collective-permute-start | bytes 417800 | tf_op jit(solution)/shard_map/ppermute | solution.py:106
  7.7 12.3 %collective-permute-start.1 = (bf16[272,256]{1,0:T(8,128)(2,1)S(1)}, bf16[272,256]{1,0:T(8,128)(2,1)S(1)}, u32[]{:S(2)}, u32[]{:S(2)}) collective-permute-start(bf16[272,256]{1,0:T(8,128)(2,1)S(1)} %pad_maximum_fusion.refs_4_), channel_id=1, source_target_pairs={{0,3},{1,4},{2,5},{3,6},{4,7},{5,8},{6,9},{7,10},{8,11},{9,12},{10... | collective-permute-start | bytes 417800 | tf_op jit(solution)/shard_map/ppermute | solution.py:106
  12.2 8.1 %collective-permute-start = (bf16[272,256]{1,0:T(8,128)(2,1)S(1)}, bf16[272,256]{1,0:T(8,128)(2,1)S(1)}, u32[]{:S(2)}, u32[]{:S(2)}) collective-permute-start(bf16[272,256]{1,0:T(8,128)(2,1)S(1)} %pad_maximum_fusion.refs_4_), channel_id=1, source_target_pairs={{0,4},{1,5},{2,6},{3,7},{4,8},{5,9},{6,10},{7,11},{8,12},{9,13},{1... | collective-permute-start | bytes 417800 | tf_op jit(solution)/shard_map/ppermute | solution.py:106
  17.0 0.7 copy-start.6
  18.5 0.7 copy-start.5
  20.0 0.7 copy-start.1
  20.0 0.7 copy-start.2
  20.0 0.7 copy-start.3
  20.2 0.6 copy-start.4
  31.1 0.7 copy-start.7
  62.0 0.5 copy-start.8

commit v4 on v3

--- a/solution.py
+++ b/solution.py
@@ -88,6 +88,12 @@
     )(here, *pieces, q, qseg, spans, readout)
 
 
+def gathered(value, axes):
+    count = lax.axis_size(axes)
+    copies = jnp.broadcast_to(value[None], (count,) + value.shape)
+    return lax.all_to_all(copies, axes, 0, 0, tiled=False)
+
+
 def per_device(queries, keys, values, segment_ids, span_ids, readout):
     tok = queries.shape[1]
     head_dim = keys.shape[2]
@@ -110,8 +116,8 @@
         jnp.reshape(here, (1,)).astype(jnp.int32), pieces, queries[0],
         qseg.astype(jnp.float32)[:, None], span_ids[0][:, None], readout[None, :],
     )
-    span_scores = lax.psum(lax.all_gather(part[0], "ctx").sum(0), "phase")
-    every = lax.all_gather(span_scores, "dp")
+    span_scores = gathered(part[0], ("phase", "ctx")).sum(0)
+    every = gathered(span_scores, "dp")
     pair_loss = jnp.mean(jax.nn.softplus(-(every[:, 0] - every[:, 1])))
     return (attended[None], span_scores[None], pair_loss)
 

time: 97.7 us -> 83.6 us (0.86)
  the two profiles are of different devices: /device:TPU:2 before, /device:TPU:1 now
where the time goes in v4:
time: 83.6 us; the launch traced here: 83.2 us
  blocking collectives  47.2 us (56%)
  starting transfers between devices  15.5 us (19%)
  Pallas kernels  10.2 us (12%)
  local copies, waits for them, and re-layouts  4.88 us (6%)
  between operations  2.51 us (3%)
  other arithmetic  2.3 us (3%)
    all_to_all x2, blocking collectives, gathered(): return lax.all_to_all(copies, axes, 0, 0, tiled=False)  47.2 us
    ppermute x4, starting transfers between devices, per_device(): pieces.append(lax.ppermute(packed, 'ctx', pairs))  15.5 us
    pallas_call x1, Pallas kernels, attend(): pl.pallas_call(attend_kernel, grid_spec=grid_spec, out_shape=[jax.ShapeDt...  10.2 us
    unnamed x18, local copies, waits for them, and re-layouts  3.16 us
  transfers between devices with their start and end apart: 4, of which 1 were waited for; matrix products, arithmetic and copies ran while one was open for 2% of the time, Pallas kernels for 0%

profile of v4, /device:TPU:1, one launch (start us, length us, event | category | flops | bytes accessed | tf_op | source)
XLA Modules:
  0.0 83.2 jit_solution(11714951712262681686)
XLA Ops:
  0.6 0.7 convert_reduce_fusion
  1.3 0.9 %pad_maximum_fusion.refs_4_ = bf16[272,256]{1,0:T(8,128)(2,1)S(1)} fusion(bf16[16,256]{1,0:T(8,128)(2,1)S(1)} %broadcast_in_dim.30, bf16[256,128]{1,0:T(8,128)(2,1)} %bitcast.29, bf16[256,128]{1,0:T(8,128)(2,1)} %bitcast.30), kind=kLoop, calls=%fused_computation | loop fusion | flops 417792 | bytes 278528 | tf_op jit(solution)/shard_map/concatenate | solution.py:108
  2.2 0.0 copy-start
  2.2 4.6 %collective-permute-start.3 = (bf16[272,256]{1,0:T(8,128)(2,1)S(1)}, bf16[272,256]{1,0:T(8,128)(2,1)S(1)}, u32[]{:S(2)}, u32[]{:S(2)}) collective-permute-start(bf16[272,256]{1,0:T(8,128)(2,1)S(1)} %pad_maximum_fusion.refs_4_), channel_id=1, source_target_pairs={{0,1},{1,2},{2,3},{3,4},{4,5},{5,6},{6,7},{7,8},{8,9},{9,10},{10,1... | collective-permute-start | bytes 417800 | tf_op jit(solution)/shard_map/ppermute | solution.py:112
  6.8 3.2 %collective-permute-start.2 = (bf16[272,256]{1,0:T(8,128)(2,1)S(1)}, bf16[272,256]{1,0:T(8,128)(2,1)S(1)}, u32[]{:S(2)}, u32[]{:S(2)}) collective-permute-start(bf16[272,256]{1,0:T(8,128)(2,1)S(1)} %pad_maximum_fusion.refs_4_), channel_id=1, source_target_pairs={{0,2},{1,3},{2,4},{3,5},{4,6},{5,7},{6,8},{7,9},{8,10},{9,11},{10,... | collective-permute-start | bytes 417800 | tf_op jit(solution)/shard_map/ppermute | solution.py:112
  10.0 3.2 %collective-permute-start.1 = (bf16[272,256]{1,0:T(8,128)(2,1)S(1)}, bf16[272,256]{1,0:T(8,128)(2,1)S(1)}, u32[]{:S(2)}, u32[]{:S(2)}) collective-permute-start(bf16[272,256]{1,0:T(8,128)(2,1)S(1)} %pad_maximum_fusion.refs_4_), channel_id=1, source_target_pairs={{0,3},{1,4},{2,5},{3,6},{4,7},{5,8},{6,9},{7,10},{8,11},{9,12},{10... | collective-permute-start | bytes 417800 | tf_op jit(solution)/shard_map/ppermute | solution.py:112
  13.3 4.5 %collective-permute-start = (bf16[272,256]{1,0:T(8,128)(2,1)S(1)}, bf16[272,256]{1,0:T(8,128)(2,1)S(1)}, u32[]{:S(2)}, u32[]{:S(2)}) collective-permute-start(bf16[272,256]{1,0:T(8,128)(2,1)S(1)} %pad_maximum_fusion.refs_4_), channel_id=1, source_target_pairs={{0,4},{1,5},{2,6},{3,7},{4,8},{5,9},{6,10},{7,11},{8,12},{9,13},{1... | collective-permute-start | bytes 417800 | tf_op jit(solution)/shard_map/ppermute | solution.py:112
  17.8 0.0 copy-start.7
  17.8 0.7 copy-done.7
  18.5 0.8 copy.17.refs_6_
  19.3 0.0 copy-start.6
  19.3 0.7 copy-done.6
  20.0 0.8 copy.18.refs_7_
  20.8 0.0 collective-permute-done.3.refs_3_
  20.8 0.0 collective-permute-done.2.refs_2_
  20.8 0.0 copy-start.2
  20.8 0.0 collective-permute-done.1.refs_1_
  20.8 0.0 copy-start.3
  20.8 0.5 collective-permute-done.refs_0_
  21.3 0.0 copy-done
  21.3 0.1 copy-done.1
  21.4 0.1 copy-done.2
  21.5 0.0 copy-done.3
  21.5 0.4 copy-done.4
  22.0 10.2 %shard_map.85 = (bf16[256,1024]{1,0:T(8,128)(2,1)}, f32[1,2]{1,0:T(1,128)}) custom-call(s32[1]{0:T(128)} %bitcast.here_ref, bf16[272,256]{1,0:T(8,128)(2,1)} %copy-done.4, bf16[272,256]{1,0:T(8,128)(2,1)} %copy-done.3, bf16[272,256]{1,0:T(8,128)(2,1)} %copy-done.2, bf16[272,256]{1,0:T(8,128)(2,1)} %copy-done.1, bf16[272,256]{1,0:T(8,128)(2,1)} %copy-done, ...), custom_call_target="tpu_custom_call" | custom-call | tf_op jit(solution)/shard_map/pallas_call | solution.py:79
  32.2 0.7 copy-done.8
  32.9 23.6 %all_to_all.15 = f32[64,1,2]{2,1,0:T(1,128)S(1)} all-to-all(f32[64,1,2]{2,1,0:T(1,128)S(1)} %broadcast_in_dim.33), channel_id=1, replica_groups=mesh['dp'=12,'phase'=4,'ctx'=16] {'phase','ctx'}, dimensions={0} | all-to-all | bytes 1024 | tf_op jit(solution)/shard_map/all_to_all | solution.py:94
  56.5 0.1 reduce_sum.18
  56.6 0.5 copy-done.5
  57.1 23.6 %all_to_all.16 = f32[12,1,2]{2,1,0:T(1,128)S(1)} all-to-all(f32[12,1,2]{2,1,0:T(1,128)S(1)} %broadcast_in_dim.35), channel_id=1, replica_groups=mesh['dp'=12,'phase'=4,'ctx'=16] {'dp'}, dimensions={0} | all-to-all | bytes 192 | tf_op jit(solution)/shard_map/all_to_all | solution.py:94
  80.7 0.1 copy.20
  80.8 0.6 fusion
  (8 shorter events, 0.0 us)
Async XLA Ops:
  2.2 19.1 %copy-start = (bf16[272,256]{1,0:T(8,128)(2,1)}, bf16[272,256]{1,0:T(8,128)(2,1)S(1)}, u32[]{:S(2)}) copy-start(bf16[272,256]{1,0:T(8,128)(2,1)S(1)} %pad_maximum_fusion.refs_4_) | copy-start | bytes 417796
  2.2 18.5 %collective-permute-start.3 = (bf16[272,256]{1,0:T(8,128)(2,1)S(1)}, bf16[272,256]{1,0:T(8,128)(2,1)S(1)}, u32[]{:S(2)}, u32[]{:S(2)}) collective-permute-start(bf16[272,256]{1,0:T(8,128)(2,1)S(1)} %pad_maximum_fusion.refs_4_), channel_id=1, source_target_pairs={{0,1},{1,2},{2,3},{3,4},{4,5},{5,6},{6,7},{7,8},{8,9},{9,10},{10,1... | collective-permute-start | bytes 417800 | tf_op jit(solution)/shard_map/ppermute | solution.py:112
  6.8 14.0 %collective-permute-start.2 = (bf16[272,256]{1,0:T(8,128)(2,1)S(1)}, bf16[272,256]{1,0:T(8,128)(2,1)S(1)}, u32[]{:S(2)}, u32[]{:S(2)}) collective-permute-start(bf16[272,256]{1,0:T(8,128)(2,1)S(1)} %pad_maximum_fusion.refs_4_), channel_id=1, source_target_pairs={{0,2},{1,3},{2,4},{3,5},{4,6},{5,7},{6,8},{7,9},{8,10},{9,11},{10,... | collective-permute-start | bytes 417800 | tf_op jit(solution)/shard_map/ppermute | solution.py:112
  10.0 10.8 %collective-permute-start.1 = (bf16[272,256]{1,0:T(8,128)(2,1)S(1)}, bf16[272,256]{1,0:T(8,128)(2,1)S(1)}, u32[]{:S(2)}, u32[]{:S(2)}) collective-permute-start(bf16[272,256]{1,0:T(8,128)(2,1)S(1)} %pad_maximum_fusion.refs_4_), channel_id=1, source_target_pairs={{0,3},{1,4},{2,5},{3,6},{4,7},{5,8},{6,9},{7,10},{8,11},{9,12},{10... | collective-permute-start | bytes 417800 | tf_op jit(solution)/shard_map/ppermute | solution.py:112
  13.3 8.0 %collective-permute-start = (bf16[272,256]{1,0:T(8,128)(2,1)S(1)}, bf16[272,256]{1,0:T(8,128)(2,1)S(1)}, u32[]{:S(2)}, u32[]{:S(2)}) collective-permute-start(bf16[272,256]{1,0:T(8,128)(2,1)S(1)} %pad_maximum_fusion.refs_4_), channel_id=1, source_target_pairs={{0,4},{1,5},{2,6},{3,7},{4,8},{5,9},{6,10},{7,11},{8,12},{9,13},{1... | collective-permute-start | bytes 417800 | tf_op jit(solution)/shard_map/ppermute | solution.py:112
  17.8 0.7 copy-start.7
  19.3 0.7 copy-start.6
  20.8 0.7 copy-start.1
  20.8 0.7 copy-start.2
  20.8 0.7 copy-start.3
  21.3 0.6 copy-start.4
  32.2 0.7 copy-start.8
  56.6 0.5 copy-start.5

commit v5 on v4

--- a/solution.py
+++ b/solution.py
@@ -10,70 +10,58 @@
 
 
 def attend_kernel(here_ref, *refs):
-    npieces = len(refs) - 10
+    npieces = len(refs) - 8
     pieces = refs[:npieces]
-    q_ref, qseg_ref, span_ref, r_ref, o_ref, part_ref, k_all, v_all, bias, score = refs[npieces:]
-    h = pl.program_id(0)
-    tok, hd = q_ref.shape
-
-    @pl.when(h == 0)
-    def _():
-        here = here_ref[0]
-        qpos = here * tok + lax.broadcasted_iota(jnp.int32, (tok, 1), 0)
-        qseg = qseg_ref[...]
-        for i, p_ref in enumerate(pieces):
-            k_all[pl.ds(i * tok, tok), :] = p_ref[pl.ds(0, tok), pl.ds(0, hd)]
-            v_all[pl.ds(i * tok, tok), :] = p_ref[pl.ds(0, tok), pl.ds(hd, hd)]
-            kseg = p_ref[pl.ds(tok, 16), pl.ds(0, tok)].astype(jnp.float32)[0:1, :]
-            kpos = (here - (npieces - 1 - i)) * tok + lax.broadcasted_iota(jnp.int32, (1, tok), 1)
-            allow = (kpos <= qpos) & (kpos >= 0) & (kseg == qseg)
-            bias[:, pl.ds(i * tok, tok)] = jnp.where(allow, 0.0, MASKED)
-        score[...] = jnp.zeros_like(score)
-
+    q_ref, qseg_ref, span_ref, r_ref, o_ref, part_ref, k_all, v_all = refs[npieces:]
+    tok, width = q_ref.shape
+    hd = k_all.shape[1]
+    here = here_ref[0]
+    qpos = here * tok + lax.broadcasted_iota(jnp.int32, (tok, 1), 0)
+    qseg = qseg_ref[...]
+    biases = []
+    for i, p_ref in enumerate(pieces):
+        k_all[pl.ds(i * tok, tok), :] = p_ref[pl.ds(0, tok), pl.ds(0, hd)]
+        v_all[pl.ds(i * tok, tok), :] = p_ref[pl.ds(0, tok), pl.ds(hd, hd)]
+        kseg = p_ref[pl.ds(tok, 16), pl.ds(0, tok)].astype(jnp.float32)[0:1, :]
+        kpos = (here - (npieces - 1 - i)) * tok + lax.broadcasted_iota(jnp.int32, (1, tok), 1)
+        allow = (kpos <= qpos) & (kpos >= 0) & (kseg == qseg)
+        biases.append(jnp.where(allow, 0.0, MASKED))
+    bias = jnp.concatenate(biases, axis=1)
     scale = 1.0 / jnp.sqrt(jnp.float32(hd))
-    sc = lax.dot_general(
-        q_ref[...], k_all[...], (((1,), (1,)), ((), ())), preferred_element_type=jnp.float32
-    )
-    sc = sc * scale + bias[...]
-    top = jnp.max(sc, axis=1, keepdims=True)
-    prob = jnp.exp(sc - top)
-    total = jnp.sum(prob, axis=1, keepdims=True)
-    acc = jnp.dot(prob.astype(jnp.bfloat16), v_all[...], preferred_element_type=jnp.float32)
-    full = acc / total
-    o_ref[...] = full.astype(o_ref.dtype)
-    score[...] += jnp.sum(full * r_ref[...], axis=1, keepdims=True)
-
-    @pl.when(h == pl.num_programs(0) - 1)
-    def _():
-        spans = span_ref[...]
-        s = score[...]
-        chosen = jnp.sum(jnp.where(spans == 1, s, 0.0), axis=0, keepdims=True)
-        reject = jnp.sum(jnp.where(spans == 2, s, 0.0), axis=0, keepdims=True)
-        part_ref[...] = jnp.concatenate([chosen, reject], axis=1) / 64.0
+    score = jnp.zeros((tok, 1), jnp.float32)
+    for h in range(width // hd):
+        cols = pl.ds(h * hd, hd)
+        sc = lax.dot_general(
+            q_ref[:, cols], k_all[...], (((1,), (1,)), ((), ())), preferred_element_type=jnp.float32
+        )
+        sc = sc * scale + bias
+        top = jnp.max(sc, axis=1, keepdims=True)
+        prob = jnp.exp(sc - top)
+        total = jnp.sum(prob, axis=1, keepdims=True)
+        acc = jnp.dot(prob.astype(jnp.bfloat16), v_all[...], preferred_element_type=jnp.float32)
+        full = acc / total
+        o_ref[:, cols] = full.astype(o_ref.dtype)
+        score = score + jnp.sum(full * r_ref[:, cols], axis=1, keepdims=True)
+    spans = span_ref[...]
+    chosen = jnp.sum(jnp.where(spans == 1, score, 0.0), axis=0, keepdims=True)
+    reject = jnp.sum(jnp.where(spans == 2, score, 0.0), axis=0, keepdims=True)
+    part_ref[...] = jnp.concatenate([chosen, reject], axis=1) / 64.0
 
 
 def attend(here, pieces, q, qseg, spans, readout, interpret=False):
     tok, width = q.shape
     hd = pieces[0].shape[1] // 2
-    heads = width // hd
     n = len(pieces)
     full = lambda shape: pl.BlockSpec(shape, lambda h, here: (0, 0))
     grid_spec = pltpu.PrefetchScalarGridSpec(
         num_scalar_prefetch=1,
-        grid=(heads,),
+        grid=(1,),
         in_specs=[full(p.shape) for p in pieces]
-        + [
-            pl.BlockSpec((tok, hd), lambda h, here: (0, h)),
-            full((tok, 1)),
-            full((tok, 1)),
-            pl.BlockSpec((1, hd), lambda h, here: (0, h)),
-        ],
-        out_specs=[pl.BlockSpec((tok, hd), lambda h, here: (0, h)), full((1, 2))],
+        + [full((tok, width)), full((tok, 1)), full((tok, 1)), full((1, width))],
+        out_specs=[full((tok, width)), full((1, 2))],
         scratch_shapes=[
             pltpu.VMEM((n * tok, hd), jnp.bfloat16),
             pltpu.VMEM((n * tok, hd), jnp.bfloat16),
-            pltpu.VMEM((tok, n * tok), jnp.float32),
-            pltpu.VMEM((tok, 1), jnp.float32),
         ],
     )
     return pl.pallas_call(

time: 83.6 us -> 80.6 us (0.964)
  Pallas kernels: 10.2 us -> 7.21 us
    pallas_call x1, Pallas kernels: 10.2 us -> 7.21 us  [attend(): pl.pallas_call(attend_kernel, grid_spec=grid_spec, out_shape=[jax.ShapeDt...]
where the time goes in v5:
time: 80.6 us; the launch traced here: 80.2 us
  blocking collectives  47.2 us (59%)
  starting transfers between devices  15.5 us (19%)
  Pallas kernels  7.21 us (9%)
  local copies, waits for them, and re-layouts  4.88 us (6%)
  between operations  2.51 us (3%)
  other arithmetic  2.3 us (3%)
    all_to_all x2, blocking collectives, gathered(): return lax.all_to_all(copies, axes, 0, 0, tiled=False)  47.2 us
    ppermute x4, starting transfers between devices, per_device(): pieces.append(lax.ppermute(packed, 'ctx', pairs))  15.5 us
    pallas_call x1, Pallas kernels, attend(): pl.pallas_call(attend_kernel, grid_spec=grid_spec, out_shape=[jax.ShapeDt...  7.21 us
    unnamed x18, local copies, waits for them, and re-layouts  3.16 us
  transfers between devices with their start and end apart: 4, of which 1 were waited for; matrix products, arithmetic and copies ran while one was open for 2% of the time, Pallas kernels for 0%

profile of v5, /device:TPU:1, one launch (start us, length us, event | category | flops | bytes accessed | tf_op | source)
XLA Modules:
  0.0 80.2 jit_solution(4314668874004999352)
XLA Ops:
  0.6 0.7 convert_reduce_fusion
  1.3 0.9 %pad_maximum_fusion.refs_4_ = bf16[272,256]{1,0:T(8,128)(2,1)S(1)} fusion(bf16[16,256]{1,0:T(8,128)(2,1)S(1)} %broadcast_in_dim.30, bf16[256,128]{1,0:T(8,128)(2,1)} %bitcast.29, bf16[256,128]{1,0:T(8,128)(2,1)} %bitcast.30), kind=kLoop, calls=%fused_computation | loop fusion | flops 417792 | bytes 278528 | tf_op jit(solution)/shard_map/concatenate | solution.py:96
  2.2 0.0 copy-start
  2.2 4.6 %collective-permute-start.3 = (bf16[272,256]{1,0:T(8,128)(2,1)S(1)}, bf16[272,256]{1,0:T(8,128)(2,1)S(1)}, u32[]{:S(2)}, u32[]{:S(2)}) collective-permute-start(bf16[272,256]{1,0:T(8,128)(2,1)S(1)} %pad_maximum_fusion.refs_4_), channel_id=1, source_target_pairs={{0,1},{1,2},{2,3},{3,4},{4,5},{5,6},{6,7},{7,8},{8,9},{9,10},{10,1... | collective-permute-start | bytes 417800 | tf_op jit(solution)/shard_map/ppermute | solution.py:100
  6.8 3.2 %collective-permute-start.2 = (bf16[272,256]{1,0:T(8,128)(2,1)S(1)}, bf16[272,256]{1,0:T(8,128)(2,1)S(1)}, u32[]{:S(2)}, u32[]{:S(2)}) collective-permute-start(bf16[272,256]{1,0:T(8,128)(2,1)S(1)} %pad_maximum_fusion.refs_4_), channel_id=1, source_target_pairs={{0,2},{1,3},{2,4},{3,5},{4,6},{5,7},{6,8},{7,9},{8,10},{9,11},{10,... | collective-permute-start | bytes 417800 | tf_op jit(solution)/shard_map/ppermute | solution.py:100
  10.0 3.2 %collective-permute-start.1 = (bf16[272,256]{1,0:T(8,128)(2,1)S(1)}, bf16[272,256]{1,0:T(8,128)(2,1)S(1)}, u32[]{:S(2)}, u32[]{:S(2)}) collective-permute-start(bf16[272,256]{1,0:T(8,128)(2,1)S(1)} %pad_maximum_fusion.refs_4_), channel_id=1, source_target_pairs={{0,3},{1,4},{2,5},{3,6},{4,7},{5,8},{6,9},{7,10},{8,11},{9,12},{10... | collective-permute-start | bytes 417800 | tf_op jit(solution)/shard_map/ppermute | solution.py:100
  13.3 4.5 %collective-permute-start = (bf16[272,256]{1,0:T(8,128)(2,1)S(1)}, bf16[272,256]{1,0:T(8,128)(2,1)S(1)}, u32[]{:S(2)}, u32[]{:S(2)}) collective-permute-start(bf16[272,256]{1,0:T(8,128)(2,1)S(1)} %pad_maximum_fusion.refs_4_), channel_id=1, source_target_pairs={{0,4},{1,5},{2,6},{3,7},{4,8},{5,9},{6,10},{7,11},{8,12},{9,13},{1... | collective-permute-start | bytes 417800 | tf_op jit(solution)/shard_map/ppermute | solution.py:100
  17.8 0.0 copy-start.7
  17.8 0.7 copy-done.7
  18.5 0.8 copy.17.refs_6_
  19.3 0.0 copy-start.6
  19.3 0.7 copy-done.6
  20.0 0.8 %copy.18.refs_7_ = s32[256,1]{1,0:T(8,128)} copy(s32[256,1]{0,1:T(1,128)S(1)} %bitcast.33) | data formatting | bytes 2048 | tf_op jit(solution)/shard_map/broadcast_in_dim;squeeze | solution.py:105
  20.8 0.0 collective-permute-done.3.refs_3_
  20.8 0.0 collective-permute-done.2.refs_2_
  20.8 0.0 copy-start.2
  20.8 0.0 collective-permute-done.1.refs_1_
  20.8 0.0 copy-start.3
  20.8 0.5 collective-permute-done.refs_0_
  21.3 0.0 copy-done
  21.3 0.1 copy-done.1
  21.4 0.1 copy-done.2
  21.5 0.0 copy-done.3
  21.5 0.4 copy-done.4
  22.0 7.2 %shard_map.85 = (bf16[256,1024]{1,0:T(8,128)(2,1)}, f32[1,2]{1,0:T(1,128)}) custom-call(s32[1]{0:T(128)} %bitcast.here_ref, bf16[272,256]{1,0:T(8,128)(2,1)} %copy-done.4, bf16[272,256]{1,0:T(8,128)(2,1)} %copy-done.3, bf16[272,256]{1,0:T(8,128)(2,1)} %copy-done.2, bf16[272,256]{1,0:T(8,128)(2,1)} %copy-done.1, bf16[272,256]{1,0:T(8,128)(2,1)} %copy-done, ...), custom_call_target="tpu_custom_call" | custom-call | tf_op jit(solution)/shard_map/pallas_call | solution.py:67
  29.2 0.7 copy-done.8
  29.9 23.6 %all_to_all.15 = f32[64,1,2]{2,1,0:T(1,128)S(1)} all-to-all(f32[64,1,2]{2,1,0:T(1,128)S(1)} %broadcast_in_dim.33), channel_id=1, replica_groups=mesh['dp'=12,'phase'=4,'ctx'=16] {'phase','ctx'}, dimensions={0} | all-to-all | bytes 1024 | tf_op jit(solution)/shard_map/all_to_all | solution.py:82
  53.5 0.1 reduce_sum.18
  53.6 0.5 copy-done.5
  54.1 23.6 %all_to_all.16 = f32[12,1,2]{2,1,0:T(1,128)S(1)} all-to-all(f32[12,1,2]{2,1,0:T(1,128)S(1)} %broadcast_in_dim.35), channel_id=1, replica_groups=mesh['dp'=12,'phase'=4,'ctx'=16] {'dp'}, dimensions={0} | all-to-all | bytes 192 | tf_op jit(solution)/shard_map/all_to_all | solution.py:82
  77.7 0.1 copy.20
  77.8 0.6 fusion
  (8 shorter events, 0.0 us)
Async XLA Ops:
  2.2 19.1 %copy-start = (bf16[272,256]{1,0:T(8,128)(2,1)}, bf16[272,256]{1,0:T(8,128)(2,1)S(1)}, u32[]{:S(2)}) copy-start(bf16[272,256]{1,0:T(8,128)(2,1)S(1)} %pad_maximum_fusion.refs_4_) | copy-start | bytes 417796
  2.2 18.5 %collective-permute-start.3 = (bf16[272,256]{1,0:T(8,128)(2,1)S(1)}, bf16[272,256]{1,0:T(8,128)(2,1)S(1)}, u32[]{:S(2)}, u32[]{:S(2)}) collective-permute-start(bf16[272,256]{1,0:T(8,128)(2,1)S(1)} %pad_maximum_fusion.refs_4_), channel_id=1, source_target_pairs={{0,1},{1,2},{2,3},{3,4},{4,5},{5,6},{6,7},{7,8},{8,9},{9,10},{10,1... | collective-permute-start | bytes 417800 | tf_op jit(solution)/shard_map/ppermute | solution.py:100
  6.8 14.0 %collective-permute-start.2 = (bf16[272,256]{1,0:T(8,128)(2,1)S(1)}, bf16[272,256]{1,0:T(8,128)(2,1)S(1)}, u32[]{:S(2)}, u32[]{:S(2)}) collective-permute-start(bf16[272,256]{1,0:T(8,128)(2,1)S(1)} %pad_maximum_fusion.refs_4_), channel_id=1, source_target_pairs={{0,2},{1,3},{2,4},{3,5},{4,6},{5,7},{6,8},{7,9},{8,10},{9,11},{10,... | collective-permute-start | bytes 417800 | tf_op jit(solution)/shard_map/ppermute | solution.py:100
  10.0 10.8 %collective-permute-start.1 = (bf16[272,256]{1,0:T(8,128)(2,1)S(1)}, bf16[272,256]{1,0:T(8,128)(2,1)S(1)}, u32[]{:S(2)}, u32[]{:S(2)}) collective-permute-start(bf16[272,256]{1,0:T(8,128)(2,1)S(1)} %pad_maximum_fusion.refs_4_), channel_id=1, source_target_pairs={{0,3},{1,4},{2,5},{3,6},{4,7},{5,8},{6,9},{7,10},{8,11},{9,12},{10... | collective-permute-start | bytes 417800 | tf_op jit(solution)/shard_map/ppermute | solution.py:100
  13.3 8.0 %collective-permute-start = (bf16[272,256]{1,0:T(8,128)(2,1)S(1)}, bf16[272,256]{1,0:T(8,128)(2,1)S(1)}, u32[]{:S(2)}, u32[]{:S(2)}) collective-permute-start(bf16[272,256]{1,0:T(8,128)(2,1)S(1)} %pad_maximum_fusion.refs_4_), channel_id=1, source_target_pairs={{0,4},{1,5},{2,6},{3,7},{4,8},{5,9},{6,10},{7,11},{8,12},{9,13},{1... | collective-permute-start | bytes 417800 | tf_op jit(solution)/shard_map/ppermute | solution.py:100
  17.8 0.7 copy-start.7
  19.3 0.7 copy-start.6
  20.8 0.7 copy-start.1
  20.8 0.7 copy-start.2
  20.8 0.7 copy-start.3
  21.3 0.6 copy-start.4
  29.2 0.7 copy-start.8
  53.5 0.5 copy-start.5

commit v6 on v5

--- a/solution.py
+++ b/solution.py
@@ -10,14 +10,21 @@
 
 
 def attend_kernel(here_ref, *refs):
-    npieces = len(refs) - 8
+    npieces = len(refs) - 6
     pieces = refs[:npieces]
-    q_ref, qseg_ref, span_ref, r_ref, o_ref, part_ref, k_all, v_all = refs[npieces:]
+    q_ref, r_ref, o_ref, part_ref, k_all, v_all = refs[npieces:]
     tok, width = q_ref.shape
     hd = k_all.shape[1]
     here = here_ref[0]
     qpos = here * tok + lax.broadcasted_iota(jnp.int32, (tok, 1), 0)
-    qseg = qseg_ref[...]
+    rows = pieces[-1][pl.ds(tok, 16), pl.ds(0, tok)].astype(jnp.float32)
+    half = 64
+    both = jnp.concatenate(
+        [jnp.broadcast_to(rows[0:1], (half, tok)), jnp.broadcast_to(rows[1:2], (half, tok))], axis=0
+    )
+    cols = jnp.transpose(both)
+    qseg = cols[:, 0:1]
+    spans = cols[:, half : half + 1]
     biases = []
     for i, p_ref in enumerate(pieces):
         k_all[pl.ds(i * tok, tok), :] = p_ref[pl.ds(0, tok), pl.ds(0, hd)]
@@ -42,13 +49,12 @@
         full = acc / total
         o_ref[:, cols] = full.astype(o_ref.dtype)
         score = score + jnp.sum(full * r_ref[:, cols], axis=1, keepdims=True)
-    spans = span_ref[...]
     chosen = jnp.sum(jnp.where(spans == 1, score, 0.0), axis=0, keepdims=True)
     reject = jnp.sum(jnp.where(spans == 2, score, 0.0), axis=0, keepdims=True)
     part_ref[...] = jnp.concatenate([chosen, reject], axis=1) / 64.0
 
 
-def attend(here, pieces, q, qseg, spans, readout, interpret=False):
+def attend(here, pieces, q, readout, interpret=False):
     tok, width = q.shape
     hd = pieces[0].shape[1] // 2
     n = len(pieces)
@@ -57,7 +63,7 @@
         num_scalar_prefetch=1,
         grid=(1,),
         in_specs=[full(p.shape) for p in pieces]
-        + [full((tok, width)), full((tok, 1)), full((tok, 1)), full((1, width))],
+        + [full((tok, width)), full((1, width))],
         out_specs=[full((tok, width)), full((1, 2))],
         scratch_shapes=[
             pltpu.VMEM((n * tok, hd), jnp.bfloat16),
@@ -73,7 +79,7 @@
         ],
         compiler_params=pltpu.CompilerParams(dimension_semantics=("arbitrary",)),
         interpret=interpret,
-    )(here, *pieces, q, qseg, spans, readout)
+    )(here, *pieces, q, readout)
 
 
 def gathered(value, axes):
@@ -91,7 +97,8 @@
     qseg = segment_ids[0]
 
     kv = jnp.concatenate([keys[0], values[0]], axis=1)
-    segrow = jnp.broadcast_to(qseg.astype(jnp.bfloat16)[None, :], (16, tok))
+    ids = jnp.stack([qseg, span_ids[0]]).astype(jnp.bfloat16)
+    segrow = jnp.concatenate([ids, jnp.zeros((14, tok), jnp.bfloat16)], axis=0)
     segrow = jnp.pad(segrow, ((0, 0), (0, 2 * head_dim - tok))) if tok < 2 * head_dim else segrow[:, : 2 * head_dim]
     packed = jnp.concatenate([kv, segrow], axis=0)
     pieces = []
@@ -101,8 +108,7 @@
     pieces.append(packed)
 
     attended, part = attend(
-        jnp.reshape(here, (1,)).astype(jnp.int32), pieces, queries[0],
-        qseg.astype(jnp.float32)[:, None], span_ids[0][:, None], readout[None, :],
+        jnp.reshape(here, (1,)).astype(jnp.int32), pieces, queries[0], readout[None, :]
     )
     span_scores = gathered(part[0], ("phase", "ctx")).sum(0)
     every = gathered(span_scores, "dp")

time: 80.6 us -> 80.6 us (level)
  waiting for transfers between devices: 0.51 us -> 3.45 us
  local copies, waits for them, and re-layouts: 4.88 us -> 2 us
    ppermute x4, waiting for transfers between devices: 0.51 us -> 3.45 us  [per_device(): pieces.append(lax.ppermute(packed, 'ctx', pairs))]
    unnamed x18 -> x16, local copies, waits for them, and re-layouts: 3.16 us -> 1.8 us
    another operation x1 -> x0, local copies, waits for them, and re-layouts: 0.81 us -> none  [per_device(): span_ids[0][:, None]]
  transfers between devices with their start and end apart: 4 -> 4, of which waited for: 1 -> 1; matrix products, arithmetic and copies ran while one was open for 2% -> 0% of each run, Pallas kernels for 0% -> 0%
where the time goes in v6:
time: 80.6 us; the launch traced here: 80.3 us
  blocking collectives  47.2 us (59%)
  starting transfers between devices  15.5 us (19%)
  Pallas kernels  7.13 us (9%)
  waiting for transfers between devices  3.45 us (4%)
  between operations  2.55 us (3%)
  other arithmetic  2.37 us (3%)
  local copies, waits for them, and re-layouts  2 us (2%)
    all_to_all x2, blocking collectives, gathered(): return lax.all_to_all(copies, axes, 0, 0, tiled=False)  47.2 us
    ppermute x4, starting transfers between devices, per_device(): pieces.append(lax.ppermute(packed, 'ctx', pairs))  15.5 us
    pallas_call x1, Pallas kernels, attend(): pl.pallas_call(attend_kernel, grid_spec=grid_spec, out_shape=[jax.ShapeDt...  7.13 us
    ppermute x4, waiting for transfers between devices, per_device(): pieces.append(lax.ppermute(packed, 'ctx', pairs))  3.45 us
    unnamed x16, local copies, waits for them, and re-layouts  1.8 us
  transfers between devices with their start and end apart: 4, of which 1 were waited for; matrix products, arithmetic and copies ran while one was open for 0% of the time, Pallas kernels for 0%

profile of v6, /device:TPU:1, one launch (start us, length us, event | category | flops | bytes accessed | tf_op | source)
XLA Modules:
  0.0 80.3 jit_solution(11766913532728152989)
XLA Ops:
  0.6 0.0 copy-start.6
  0.6 0.7 convert.6
  1.3 0.0 copy-done.6
  1.3 0.1 pad.4.clone
  1.4 1.0 %maximum_maximum_fusion.refs_4_ = bf16[272,256]{1,0:T(8,128)(2,1)S(1)} fusion(bf16[1,256]{1,0:T(2,128)(2,1)S(1)} %convert.7, bf16[1,256]{1,0:T(2,128)(2,1)S(1)} %convert.6, bf16[256,128]{1,0:T(8,128)(2,1)} %bitcast.26, bf16[256,128]{1,0:T(8,128)(2,1)} %bitcast.27, bf16[272]{0:T(512)(128)(2,1)S(1)} %pad.4.clone), kind=kLoop, calls=%fused_computation | loop fusion | flops 696320 | bytes 271904 | tf_op jit(solution)/shard_map/concatenate | solution.py:103
  2.4 0.0 copy-start
  2.4 4.6 %collective-permute-start.3 = (bf16[272,256]{1,0:T(8,128)(2,1)S(1)}, bf16[272,256]{1,0:T(8,128)(2,1)S(1)}, u32[]{:S(2)}, u32[]{:S(2)}) collective-permute-start(bf16[272,256]{1,0:T(8,128)(2,1)S(1)} %maximum_maximum_fusion.refs_4_), channel_id=1, source_target_pairs={{0,1},{1,2},{2,3},{3,4},{4,5},{5,6},{6,7},{7,8},{8,9},{9,10},{10,1... | collective-permute-start | bytes 417800 | tf_op jit(solution)/shard_map/ppermute | solution.py:107
  7.0 3.2 %collective-permute-start.2 = (bf16[272,256]{1,0:T(8,128)(2,1)S(1)}, bf16[272,256]{1,0:T(8,128)(2,1)S(1)}, u32[]{:S(2)}, u32[]{:S(2)}) collective-permute-start(bf16[272,256]{1,0:T(8,128)(2,1)S(1)} %maximum_maximum_fusion.refs_4_), channel_id=1, source_target_pairs={{0,2},{1,3},{2,4},{3,5},{4,6},{5,7},{6,8},{7,9},{8,10},{9,11},{10,... | collective-permute-start | bytes 417800 | tf_op jit(solution)/shard_map/ppermute | solution.py:107
  10.2 3.2 %collective-permute-start.1 = (bf16[272,256]{1,0:T(8,128)(2,1)S(1)}, bf16[272,256]{1,0:T(8,128)(2,1)S(1)}, u32[]{:S(2)}, u32[]{:S(2)}) collective-permute-start(bf16[272,256]{1,0:T(8,128)(2,1)S(1)} %maximum_maximum_fusion.refs_4_), channel_id=1, source_target_pairs={{0,3},{1,4},{2,5},{3,6},{4,7},{5,8},{6,9},{7,10},{8,11},{9,12},{10... | collective-permute-start | bytes 417800 | tf_op jit(solution)/shard_map/ppermute | solution.py:107
  13.4 4.5 %collective-permute-start = (bf16[272,256]{1,0:T(8,128)(2,1)S(1)}, bf16[272,256]{1,0:T(8,128)(2,1)S(1)}, u32[]{:S(2)}, u32[]{:S(2)}) collective-permute-start(bf16[272,256]{1,0:T(8,128)(2,1)S(1)} %maximum_maximum_fusion.refs_4_), channel_id=1, source_target_pairs={{0,4},{1,5},{2,6},{3,7},{4,8},{5,9},{6,10},{7,11},{8,12},{9,13},{1... | collective-permute-start | bytes 417800 | tf_op jit(solution)/shard_map/ppermute | solution.py:107
  18.0 0.0 collective-permute-done.3.refs_3_
  18.0 0.0 copy-start.1
  18.0 0.0 collective-permute-done.2.refs_2_
  18.0 0.0 copy-start.2
  18.0 0.0 collective-permute-done.1.refs_1_
  18.0 0.0 copy-start.3
  18.0 3.4 %collective-permute-done.refs_0_ = bf16[272,256]{1,0:T(8,128)(2,1)S(1)} collective-permute-done((bf16[272,256]{1,0:T(8,128)(2,1)S(1)}, bf16[272,256]{1,0:T(8,128)(2,1)S(1)}, u32[]{:S(2)}, u32[]{:S(2)}) %collective-permute-start) | collective-permute-done | bytes 139296 | tf_op jit(solution)/shard_map/ppermute | solution.py:107
  21.5 0.0 copy-start.4
  21.5 0.0 copy-done
  21.5 0.0 copy-done.1
  21.5 0.0 copy-done.2
  21.5 0.0 copy-done.3
  21.5 0.6 copy-done.4
  22.1 7.1 %shard_map.85 = (bf16[256,1024]{1,0:T(8,128)(2,1)}, f32[1,2]{1,0:T(1,128)}) custom-call(s32[1]{0:T(128)} %bitcast.here_ref, bf16[272,256]{1,0:T(8,128)(2,1)} %copy-done.4, bf16[272,256]{1,0:T(8,128)(2,1)} %copy-done.3, bf16[272,256]{1,0:T(8,128)(2,1)} %copy-done.2, bf16[272,256]{1,0:T(8,128)(2,1)} %copy-done.1, bf16[272,256]{1,0:T(8,128)(2,1)} %copy-done, ...), custom_call_target="tpu_custom_call" | custom-call | tf_op jit(solution)/shard_map/pallas_call | solution.py:73
  29.3 0.0 copy-start.7
  29.3 0.7 copy-done.7
  29.9 23.6 %all_to_all.15 = f32[64,1,2]{2,1,0:T(1,128)S(1)} all-to-all(f32[64,1,2]{2,1,0:T(1,128)S(1)} %broadcast_in_dim.26), channel_id=1, replica_groups=mesh['dp'=12,'phase'=4,'ctx'=16] {'phase','ctx'}, dimensions={0} | all-to-all | bytes 1024 | tf_op jit(solution)/shard_map/all_to_all | solution.py:88
  53.6 0.1 reduce_sum.18
  53.7 0.5 copy-done.5
  54.2 23.6 %all_to_all.16 = f32[12,1,2]{2,1,0:T(1,128)S(1)} all-to-all(f32[12,1,2]{2,1,0:T(1,128)S(1)} %broadcast_in_dim.28), channel_id=1, replica_groups=mesh['dp'=12,'phase'=4,'ctx'=16] {'dp'}, dimensions={0} | all-to-all | bytes 192 | tf_op jit(solution)/shard_map/all_to_all | solution.py:88
  77.8 0.1 copy.12
  77.9 0.6 fusion
  (5 shorter events, 0.0 us)
Async XLA Ops:
  0.6 0.7 copy-start.6
  2.4 19.1 %copy-start = (bf16[272,256]{1,0:T(8,128)(2,1)}, bf16[272,256]{1,0:T(8,128)(2,1)S(1)}, u32[]{:S(2)}) copy-start(bf16[272,256]{1,0:T(8,128)(2,1)S(1)} %maximum_maximum_fusion.refs_4_) | copy-start | bytes 417796
  2.4 15.6 %collective-permute-start.3 = (bf16[272,256]{1,0:T(8,128)(2,1)S(1)}, bf16[272,256]{1,0:T(8,128)(2,1)S(1)}, u32[]{:S(2)}, u32[]{:S(2)}) collective-permute-start(bf16[272,256]{1,0:T(8,128)(2,1)S(1)} %maximum_maximum_fusion.refs_4_), channel_id=1, source_target_pairs={{0,1},{1,2},{2,3},{3,4},{4,5},{5,6},{6,7},{7,8},{8,9},{9,10},{10,1... | collective-permute-start | bytes 417800 | tf_op jit(solution)/shard_map/ppermute | solution.py:107
  7.0 11.0 %collective-permute-start.2 = (bf16[272,256]{1,0:T(8,128)(2,1)S(1)}, bf16[272,256]{1,0:T(8,128)(2,1)S(1)}, u32[]{:S(2)}, u32[]{:S(2)}) collective-permute-start(bf16[272,256]{1,0:T(8,128)(2,1)S(1)} %maximum_maximum_fusion.refs_4_), channel_id=1, source_target_pairs={{0,2},{1,3},{2,4},{3,5},{4,6},{5,7},{6,8},{7,9},{8,10},{9,11},{10,... | collective-permute-start | bytes 417800 | tf_op jit(solution)/shard_map/ppermute | solution.py:107
  10.2 7.8 %collective-permute-start.1 = (bf16[272,256]{1,0:T(8,128)(2,1)S(1)}, bf16[272,256]{1,0:T(8,128)(2,1)S(1)}, u32[]{:S(2)}, u32[]{:S(2)}) collective-permute-start(bf16[272,256]{1,0:T(8,128)(2,1)S(1)} %maximum_maximum_fusion.refs_4_), channel_id=1, source_target_pairs={{0,3},{1,4},{2,5},{3,6},{4,7},{5,8},{6,9},{7,10},{8,11},{9,12},{10... | collective-permute-start | bytes 417800 | tf_op jit(solution)/shard_map/ppermute | solution.py:107
  13.4 8.0 %collective-permute-start = (bf16[272,256]{1,0:T(8,128)(2,1)S(1)}, bf16[272,256]{1,0:T(8,128)(2,1)S(1)}, u32[]{:S(2)}, u32[]{:S(2)}) collective-permute-start(bf16[272,256]{1,0:T(8,128)(2,1)S(1)} %maximum_maximum_fusion.refs_4_), channel_id=1, source_target_pairs={{0,4},{1,5},{2,6},{3,7},{4,8},{5,9},{6,10},{7,11},{8,12},{9,13},{1... | collective-permute-start | bytes 417800 | tf_op jit(solution)/shard_map/ppermute | solution.py:107
  18.0 3.5 %copy-start.1 = (bf16[272,256]{1,0:T(8,128)(2,1)}, bf16[272,256]{1,0:T(8,128)(2,1)S(1)}, u32[]{:S(2)}) copy-start(bf16[272,256]{1,0:T(8,128)(2,1)S(1)} %collective-permute-done.3.refs_3_) | copy-start | bytes 417796
  18.0 3.5 %copy-start.2 = (bf16[272,256]{1,0:T(8,128)(2,1)}, bf16[272,256]{1,0:T(8,128)(2,1)S(1)}, u32[]{:S(2)}) copy-start(bf16[272,256]{1,0:T(8,128)(2,1)S(1)} %collective-permute-done.2.refs_2_) | copy-start | bytes 417796
  18.0 3.5 %copy-start.3 = (bf16[272,256]{1,0:T(8,128)(2,1)}, bf16[272,256]{1,0:T(8,128)(2,1)S(1)}, u32[]{:S(2)}) copy-start(bf16[272,256]{1,0:T(8,128)(2,1)S(1)} %collective-permute-done.1.refs_1_) | copy-start | bytes 417796
  21.5 0.7 copy-start.4
  29.3 0.7 copy-start.7
  53.6 0.5 copy-start.5

commit v7 on v6

--- a/solution.py
+++ b/solution.py
@@ -30,8 +30,12 @@
         k_all[pl.ds(i * tok, tok), :] = p_ref[pl.ds(0, tok), pl.ds(0, hd)]
         v_all[pl.ds(i * tok, tok), :] = p_ref[pl.ds(0, tok), pl.ds(hd, hd)]
         kseg = p_ref[pl.ds(tok, 16), pl.ds(0, tok)].astype(jnp.float32)[0:1, :]
-        kpos = (here - (npieces - 1 - i)) * tok + lax.broadcasted_iota(jnp.int32, (1, tok), 1)
-        allow = (kpos <= qpos) & (kpos >= 0) & (kseg == qseg)
+        back = npieces - 1 - i
+        if back == 0:
+            kpos = here * tok + lax.broadcasted_iota(jnp.int32, (1, tok), 1)
+            allow = (kpos <= qpos) & (kseg == qseg)
+        else:
+            allow = (kseg == qseg) & (here >= back)
         biases.append(jnp.where(allow, 0.0, MASKED))
     bias = jnp.concatenate(biases, axis=1)
     scale = 1.0 / jnp.sqrt(jnp.float32(hd))

time: 80.6 us -> 80.6 us (level)
  no operation moved by 1% of the time
where the time goes in v7:
time: 80.6 us; the launch traced here: 80.3 us
  blocking collectives  47.2 us (59%)
  starting transfers between devices  15.5 us (19%)
  Pallas kernels  7.14 us (9%)
  waiting for transfers between devices  3.45 us (4%)
  between operations  2.55 us (3%)
  other arithmetic  2.37 us (3%)
  local copies, waits for them, and re-layouts  2 us (2%)
    all_to_all x2, blocking collectives, gathered(): return lax.all_to_all(copies, axes, 0, 0, tiled=False)  47.2 us
    ppermute x4, starting transfers between devices, per_device(): pieces.append(lax.ppermute(packed, 'ctx', pairs))  15.5 us
    pallas_call x1, Pallas kernels, attend(): pl.pallas_call(attend_kernel, grid_spec=grid_spec, out_shape=[jax.ShapeDt...  7.14 us
    ppermute x4, waiting for transfers between devices, per_device(): pieces.append(lax.ppermute(packed, 'ctx', pairs))  3.45 us
    unnamed x16, local copies, waits for them, and re-layouts  1.8 us
  transfers between devices with their start and end apart: 4, of which 1 were waited for; matrix products, arithmetic and copies ran while one was open for 0% of the time, Pallas kernels for 0%

profile of v7, /device:TPU:1, one launch (start us, length us, event | category | flops | bytes accessed | tf_op | source)
XLA Modules:
  0.0 80.3 jit_solution(15862630368422537894)
XLA Ops:
  0.6 0.0 copy-start.6
  0.6 0.7 convert.6
  1.3 0.0 copy-done.6
  1.3 0.1 pad.4.clone
  1.4 1.0 %maximum_maximum_fusion.refs_4_ = bf16[272,256]{1,0:T(8,128)(2,1)S(1)} fusion(bf16[1,256]{1,0:T(2,128)(2,1)S(1)} %convert.7, bf16[1,256]{1,0:T(2,128)(2,1)S(1)} %convert.6, bf16[256,128]{1,0:T(8,128)(2,1)} %bitcast.26, bf16[256,128]{1,0:T(8,128)(2,1)} %bitcast.27, bf16[272]{0:T(512)(128)(2,1)S(1)} %pad.4.clone), kind=kLoop, calls=%fused_computation | loop fusion | flops 696320 | bytes 271904 | tf_op jit(solution)/shard_map/concatenate | solution.py:107
  2.4 0.0 copy-start
  2.4 4.6 %collective-permute-start.3 = (bf16[272,256]{1,0:T(8,128)(2,1)S(1)}, bf16[272,256]{1,0:T(8,128)(2,1)S(1)}, u32[]{:S(2)}, u32[]{:S(2)}) collective-permute-start(bf16[272,256]{1,0:T(8,128)(2,1)S(1)} %maximum_maximum_fusion.refs_4_), channel_id=1, source_target_pairs={{0,1},{1,2},{2,3},{3,4},{4,5},{5,6},{6,7},{7,8},{8,9},{9,10},{10,1... | collective-permute-start | bytes 417800 | tf_op jit(solution)/shard_map/ppermute | solution.py:111
  7.0 3.2 %collective-permute-start.2 = (bf16[272,256]{1,0:T(8,128)(2,1)S(1)}, bf16[272,256]{1,0:T(8,128)(2,1)S(1)}, u32[]{:S(2)}, u32[]{:S(2)}) collective-permute-start(bf16[272,256]{1,0:T(8,128)(2,1)S(1)} %maximum_maximum_fusion.refs_4_), channel_id=1, source_target_pairs={{0,2},{1,3},{2,4},{3,5},{4,6},{5,7},{6,8},{7,9},{8,10},{9,11},{10,... | collective-permute-start | bytes 417800 | tf_op jit(solution)/shard_map/ppermute | solution.py:111
  10.2 3.2 %collective-permute-start.1 = (bf16[272,256]{1,0:T(8,128)(2,1)S(1)}, bf16[272,256]{1,0:T(8,128)(2,1)S(1)}, u32[]{:S(2)}, u32[]{:S(2)}) collective-permute-start(bf16[272,256]{1,0:T(8,128)(2,1)S(1)} %maximum_maximum_fusion.refs_4_), channel_id=1, source_target_pairs={{0,3},{1,4},{2,5},{3,6},{4,7},{5,8},{6,9},{7,10},{8,11},{9,12},{10... | collective-permute-start | bytes 417800 | tf_op jit(solution)/shard_map/ppermute | solution.py:111
  13.4 4.5 %collective-permute-start = (bf16[272,256]{1,0:T(8,128)(2,1)S(1)}, bf16[272,256]{1,0:T(8,128)(2,1)S(1)}, u32[]{:S(2)}, u32[]{:S(2)}) collective-permute-start(bf16[272,256]{1,0:T(8,128)(2,1)S(1)} %maximum_maximum_fusion.refs_4_), channel_id=1, source_target_pairs={{0,4},{1,5},{2,6},{3,7},{4,8},{5,9},{6,10},{7,11},{8,12},{9,13},{1... | collective-permute-start | bytes 417800 | tf_op jit(solution)/shard_map/ppermute | solution.py:111
  18.0 0.0 collective-permute-done.3.refs_3_
  18.0 0.0 copy-start.1
  18.0 0.0 collective-permute-done.2.refs_2_
  18.0 0.0 copy-start.2
  18.0 0.0 collective-permute-done.1.refs_1_
  18.0 0.0 copy-start.3
  18.0 3.4 %collective-permute-done.refs_0_ = bf16[272,256]{1,0:T(8,128)(2,1)S(1)} collective-permute-done((bf16[272,256]{1,0:T(8,128)(2,1)S(1)}, bf16[272,256]{1,0:T(8,128)(2,1)S(1)}, u32[]{:S(2)}, u32[]{:S(2)}) %collective-permute-start) | collective-permute-done | bytes 139296 | tf_op jit(solution)/shard_map/ppermute | solution.py:111
  21.5 0.0 copy-start.4
  21.5 0.0 copy-done
  21.5 0.0 copy-done.1
  21.5 0.0 copy-done.2
  21.5 0.0 copy-done.3
  21.5 0.6 copy-done.4
  22.1 7.1 %shard_map.85 = (bf16[256,1024]{1,0:T(8,128)(2,1)}, f32[1,2]{1,0:T(1,128)}) custom-call(s32[1]{0:T(128)} %bitcast.here_ref, bf16[272,256]{1,0:T(8,128)(2,1)} %copy-done.4, bf16[272,256]{1,0:T(8,128)(2,1)} %copy-done.3, bf16[272,256]{1,0:T(8,128)(2,1)} %copy-done.2, bf16[272,256]{1,0:T(8,128)(2,1)} %copy-done.1, bf16[272,256]{1,0:T(8,128)(2,1)} %copy-done, ...), custom_call_target="tpu_custom_call" | custom-call | tf_op jit(solution)/shard_map/pallas_call | solution.py:77
  29.3 0.0 copy-start.7
  29.3 0.7 copy-done.7
  29.9 23.6 %all_to_all.15 = f32[64,1,2]{2,1,0:T(1,128)S(1)} all-to-all(f32[64,1,2]{2,1,0:T(1,128)S(1)} %broadcast_in_dim.26), channel_id=1, replica_groups=mesh['dp'=12,'phase'=4,'ctx'=16] {'phase','ctx'}, dimensions={0} | all-to-all | bytes 1024 | tf_op jit(solution)/shard_map/all_to_all | solution.py:92
  53.6 0.1 reduce_sum.18
  53.7 0.5 copy-done.5
  54.1 23.6 %all_to_all.16 = f32[12,1,2]{2,1,0:T(1,128)S(1)} all-to-all(f32[12,1,2]{2,1,0:T(1,128)S(1)} %broadcast_in_dim.28), channel_id=1, replica_groups=mesh['dp'=12,'phase'=4,'ctx'=16] {'dp'}, dimensions={0} | all-to-all | bytes 192 | tf_op jit(solution)/shard_map/all_to_all | solution.py:92
  77.8 0.1 copy.12
  77.9 0.6 fusion
  (5 shorter events, 0.0 us)
Async XLA Ops:
  0.6 0.7 copy-start.6
  2.4 19.1 %copy-start = (bf16[272,256]{1,0:T(8,128)(2,1)}, bf16[272,256]{1,0:T(8,128)(2,1)S(1)}, u32[]{:S(2)}) copy-start(bf16[272,256]{1,0:T(8,128)(2,1)S(1)} %maximum_maximum_fusion.refs_4_) | copy-start | bytes 417796
  2.4 15.6 %collective-permute-start.3 = (bf16[272,256]{1,0:T(8,128)(2,1)S(1)}, bf16[272,256]{1,0:T(8,128)(2,1)S(1)}, u32[]{:S(2)}, u32[]{:S(2)}) collective-permute-start(bf16[272,256]{1,0:T(8,128)(2,1)S(1)} %maximum_maximum_fusion.refs_4_), channel_id=1, source_target_pairs={{0,1},{1,2},{2,3},{3,4},{4,5},{5,6},{6,7},{7,8},{8,9},{9,10},{10,1... | collective-permute-start | bytes 417800 | tf_op jit(solution)/shard_map/ppermute | solution.py:111
  7.0 11.0 %collective-permute-start.2 = (bf16[272,256]{1,0:T(8,128)(2,1)S(1)}, bf16[272,256]{1,0:T(8,128)(2,1)S(1)}, u32[]{:S(2)}, u32[]{:S(2)}) collective-permute-start(bf16[272,256]{1,0:T(8,128)(2,1)S(1)} %maximum_maximum_fusion.refs_4_), channel_id=1, source_target_pairs={{0,2},{1,3},{2,4},{3,5},{4,6},{5,7},{6,8},{7,9},{8,10},{9,11},{10,... | collective-permute-start | bytes 417800 | tf_op jit(solution)/shard_map/ppermute | solution.py:111
  10.2 7.8 %collective-permute-start.1 = (bf16[272,256]{1,0:T(8,128)(2,1)S(1)}, bf16[272,256]{1,0:T(8,128)(2,1)S(1)}, u32[]{:S(2)}, u32[]{:S(2)}) collective-permute-start(bf16[272,256]{1,0:T(8,128)(2,1)S(1)} %maximum_maximum_fusion.refs_4_), channel_id=1, source_target_pairs={{0,3},{1,4},{2,5},{3,6},{4,7},{5,8},{6,9},{7,10},{8,11},{9,12},{10... | collective-permute-start | bytes 417800 | tf_op jit(solution)/shard_map/ppermute | solution.py:111
  13.4 8.0 %collective-permute-start = (bf16[272,256]{1,0:T(8,128)(2,1)S(1)}, bf16[272,256]{1,0:T(8,128)(2,1)S(1)}, u32[]{:S(2)}, u32[]{:S(2)}) collective-permute-start(bf16[272,256]{1,0:T(8,128)(2,1)S(1)} %maximum_maximum_fusion.refs_4_), channel_id=1, source_target_pairs={{0,4},{1,5},{2,6},{3,7},{4,8},{5,9},{6,10},{7,11},{8,12},{9,13},{1... | collective-permute-start | bytes 417800 | tf_op jit(solution)/shard_map/ppermute | solution.py:111
  18.0 3.5 %copy-start.1 = (bf16[272,256]{1,0:T(8,128)(2,1)}, bf16[272,256]{1,0:T(8,128)(2,1)S(1)}, u32[]{:S(2)}) copy-start(bf16[272,256]{1,0:T(8,128)(2,1)S(1)} %collective-permute-done.3.refs_3_) | copy-start | bytes 417796
  18.0 3.5 %copy-start.2 = (bf16[272,256]{1,0:T(8,128)(2,1)}, bf16[272,256]{1,0:T(8,128)(2,1)S(1)}, u32[]{:S(2)}) copy-start(bf16[272,256]{1,0:T(8,128)(2,1)S(1)} %collective-permute-done.2.refs_2_) | copy-start | bytes 417796
  18.0 3.5 %copy-start.3 = (bf16[272,256]{1,0:T(8,128)(2,1)}, bf16[272,256]{1,0:T(8,128)(2,1)S(1)}, u32[]{:S(2)}) copy-start(bf16[272,256]{1,0:T(8,128)(2,1)S(1)} %collective-permute-done.1.refs_1_) | copy-start | bytes 417796
  21.5 0.7 copy-start.4
  29.3 0.7 copy-start.7
  53.6 0.5 copy-start.5

commit v8 on v6

--- a/solution.py
+++ b/solution.py
@@ -10,11 +10,11 @@
 
 
 def attend_kernel(here_ref, *refs):
-    npieces = len(refs) - 6
+    npieces = len(refs) - 4
     pieces = refs[:npieces]
-    q_ref, r_ref, o_ref, part_ref, k_all, v_all = refs[npieces:]
+    q_ref, r_ref, o_ref, part_ref = refs[npieces:]
     tok, width = q_ref.shape
-    hd = k_all.shape[1]
+    hd = pieces[0].shape[1] // 2
     here = here_ref[0]
     qpos = here * tok + lax.broadcasted_iota(jnp.int32, (tok, 1), 0)
     rows = pieces[-1][pl.ds(tok, 16), pl.ds(0, tok)].astype(jnp.float32)
@@ -27,25 +27,34 @@
     spans = cols[:, half : half + 1]
     biases = []
     for i, p_ref in enumerate(pieces):
-        k_all[pl.ds(i * tok, tok), :] = p_ref[pl.ds(0, tok), pl.ds(0, hd)]
-        v_all[pl.ds(i * tok, tok), :] = p_ref[pl.ds(0, tok), pl.ds(hd, hd)]
         kseg = p_ref[pl.ds(tok, 16), pl.ds(0, tok)].astype(jnp.float32)[0:1, :]
         kpos = (here - (npieces - 1 - i)) * tok + lax.broadcasted_iota(jnp.int32, (1, tok), 1)
         allow = (kpos <= qpos) & (kpos >= 0) & (kseg == qseg)
         biases.append(jnp.where(allow, 0.0, MASKED))
-    bias = jnp.concatenate(biases, axis=1)
     scale = 1.0 / jnp.sqrt(jnp.float32(hd))
     score = jnp.zeros((tok, 1), jnp.float32)
     for h in range(width // hd):
         cols = pl.ds(h * hd, hd)
-        sc = lax.dot_general(
-            q_ref[:, cols], k_all[...], (((1,), (1,)), ((), ())), preferred_element_type=jnp.float32
-        )
-        sc = sc * scale + bias
-        top = jnp.max(sc, axis=1, keepdims=True)
-        prob = jnp.exp(sc - top)
-        total = jnp.sum(prob, axis=1, keepdims=True)
-        acc = jnp.dot(prob.astype(jnp.bfloat16), v_all[...], preferred_element_type=jnp.float32)
+        qh = q_ref[:, cols]
+        scs = []
+        for i, p_ref in enumerate(pieces):
+            sc = lax.dot_general(
+                qh, p_ref[pl.ds(0, tok), pl.ds(0, hd)], (((1,), (1,)), ((), ())),
+                preferred_element_type=jnp.float32,
+            )
+            scs.append(sc * scale + biases[i])
+        top = scs[0].max(axis=1, keepdims=True)
+        for sc in scs[1:]:
+            top = jnp.maximum(top, sc.max(axis=1, keepdims=True))
+        total = jnp.zeros((tok, 1), jnp.float32)
+        acc = jnp.zeros((tok, hd), jnp.float32)
+        for i, p_ref in enumerate(pieces):
+            prob = jnp.exp(scs[i] - top)
+            total = total + jnp.sum(prob, axis=1, keepdims=True)
+            acc = acc + jnp.dot(
+                prob.astype(jnp.bfloat16), p_ref[pl.ds(0, tok), pl.ds(hd, hd)],
+                preferred_element_type=jnp.float32,
+            )
         full = acc / total
         o_ref[:, cols] = full.astype(o_ref.dtype)
         score = score + jnp.sum(full * r_ref[:, cols], axis=1, keepdims=True)
@@ -65,10 +74,6 @@
         in_specs=[full(p.shape) for p in pieces]
         + [full((tok, width)), full((1, width))],
         out_specs=[full((tok, width)), full((1, 2))],
-        scratch_shapes=[
-            pltpu.VMEM((n * tok, hd), jnp.bfloat16),
-            pltpu.VMEM((n * tok, hd), jnp.bfloat16),
-        ],
     )
     return pl.pallas_call(
         attend_kernel,

time: 80.6 us -> 80.5 us (level)
  no operation moved by 1% of the time
where the time goes in v8:
time: 80.5 us; the launch traced here: 80.1 us
  blocking collectives  47.2 us (59%)
  starting transfers between devices  15.5 us (19%)
  Pallas kernels  6.98 us (9%)
  waiting for transfers between devices  3.45 us (4%)
  between operations  2.55 us (3%)
  other arithmetic  2.37 us (3%)
  local copies, waits for them, and re-layouts  2 us (2%)
    all_to_all x2, blocking collectives, gathered(): return lax.all_to_all(copies, axes, 0, 0, tiled=False)  47.2 us
    ppermute x4, starting transfers between devices, per_device(): pieces.append(lax.ppermute(packed, 'ctx', pairs))  15.5 us
    pallas_call x1, Pallas kernels, attend(): pl.pallas_call(attend_kernel, grid_spec=grid_spec, out_shape=[jax.ShapeDt...  6.98 us
    ppermute x4, waiting for transfers between devices, per_device(): pieces.append(lax.ppermute(packed, 'ctx', pairs))  3.45 us
    unnamed x16, local copies, waits for them, and re-layouts  1.8 us
  transfers between devices with their start and end apart: 4, of which 1 were waited for; matrix products, arithmetic and copies ran while one was open for 0% of the time, Pallas kernels for 0%

profile of v8, /device:TPU:1, one launch (start us, length us, event | category | flops | bytes accessed | tf_op | source)
XLA Modules:
  0.0 80.1 jit_solution(4872478851642094598)
XLA Ops:
  0.6 0.0 copy-start.6
  0.6 0.7 convert.6
  1.3 0.0 copy-done.6
  1.3 0.1 pad.4.clone
  1.4 1.0 %maximum_maximum_fusion.refs_4_ = bf16[272,256]{1,0:T(8,128)(2,1)S(1)} fusion(bf16[1,256]{1,0:T(2,128)(2,1)S(1)} %convert.7, bf16[1,256]{1,0:T(2,128)(2,1)S(1)} %convert.6, bf16[256,128]{1,0:T(8,128)(2,1)} %bitcast.26, bf16[256,128]{1,0:T(8,128)(2,1)} %bitcast.27, bf16[272]{0:T(512)(128)(2,1)S(1)} %pad.4.clone), kind=kLoop, calls=%fused_computation | loop fusion | flops 696320 | bytes 271904 | tf_op jit(solution)/shard_map/concatenate | solution.py:108
  2.4 0.0 copy-start
  2.4 4.6 %collective-permute-start.3 = (bf16[272,256]{1,0:T(8,128)(2,1)S(1)}, bf16[272,256]{1,0:T(8,128)(2,1)S(1)}, u32[]{:S(2)}, u32[]{:S(2)}) collective-permute-start(bf16[272,256]{1,0:T(8,128)(2,1)S(1)} %maximum_maximum_fusion.refs_4_), channel_id=1, source_target_pairs={{0,1},{1,2},{2,3},{3,4},{4,5},{5,6},{6,7},{7,8},{8,9},{9,10},{10,1... | collective-permute-start | bytes 417800 | tf_op jit(solution)/shard_map/ppermute | solution.py:112
  7.0 3.2 %collective-permute-start.2 = (bf16[272,256]{1,0:T(8,128)(2,1)S(1)}, bf16[272,256]{1,0:T(8,128)(2,1)S(1)}, u32[]{:S(2)}, u32[]{:S(2)}) collective-permute-start(bf16[272,256]{1,0:T(8,128)(2,1)S(1)} %maximum_maximum_fusion.refs_4_), channel_id=1, source_target_pairs={{0,2},{1,3},{2,4},{3,5},{4,6},{5,7},{6,8},{7,9},{8,10},{9,11},{10,... | collective-permute-start | bytes 417800 | tf_op jit(solution)/shard_map/ppermute | solution.py:112
  10.2 3.2 %collective-permute-start.1 = (bf16[272,256]{1,0:T(8,128)(2,1)S(1)}, bf16[272,256]{1,0:T(8,128)(2,1)S(1)}, u32[]{:S(2)}, u32[]{:S(2)}) collective-permute-start(bf16[272,256]{1,0:T(8,128)(2,1)S(1)} %maximum_maximum_fusion.refs_4_), channel_id=1, source_target_pairs={{0,3},{1,4},{2,5},{3,6},{4,7},{5,8},{6,9},{7,10},{8,11},{9,12},{10... | collective-permute-start | bytes 417800 | tf_op jit(solution)/shard_map/ppermute | solution.py:112
  13.4 4.5 %collective-permute-start = (bf16[272,256]{1,0:T(8,128)(2,1)S(1)}, bf16[272,256]{1,0:T(8,128)(2,1)S(1)}, u32[]{:S(2)}, u32[]{:S(2)}) collective-permute-start(bf16[272,256]{1,0:T(8,128)(2,1)S(1)} %maximum_maximum_fusion.refs_4_), channel_id=1, source_target_pairs={{0,4},{1,5},{2,6},{3,7},{4,8},{5,9},{6,10},{7,11},{8,12},{9,13},{1... | collective-permute-start | bytes 417800 | tf_op jit(solution)/shard_map/ppermute | solution.py:112
  18.0 0.0 collective-permute-done.3.refs_3_
  18.0 0.0 copy-start.1
  18.0 0.0 collective-permute-done.2.refs_2_
  18.0 0.0 copy-start.2
  18.0 0.0 collective-permute-done.1.refs_1_
  18.0 0.0 copy-start.3
  18.0 3.4 %collective-permute-done.refs_0_ = bf16[272,256]{1,0:T(8,128)(2,1)S(1)} collective-permute-done((bf16[272,256]{1,0:T(8,128)(2,1)S(1)}, bf16[272,256]{1,0:T(8,128)(2,1)S(1)}, u32[]{:S(2)}, u32[]{:S(2)}) %collective-permute-start) | collective-permute-done | bytes 139296 | tf_op jit(solution)/shard_map/ppermute | solution.py:112
  21.5 0.0 copy-start.4
  21.5 0.0 copy-done
  21.5 0.0 copy-done.1
  21.5 0.0 copy-done.2
  21.5 0.0 copy-done.3
  21.5 0.6 copy-done.4
  22.1 7.0 %shard_map.85 = (bf16[256,1024]{1,0:T(8,128)(2,1)}, f32[1,2]{1,0:T(1,128)}) custom-call(s32[1]{0:T(128)} %bitcast.here_ref, bf16[272,256]{1,0:T(8,128)(2,1)} %copy-done.4, bf16[272,256]{1,0:T(8,128)(2,1)} %copy-done.3, bf16[272,256]{1,0:T(8,128)(2,1)} %copy-done.2, bf16[272,256]{1,0:T(8,128)(2,1)} %copy-done.1, bf16[272,256]{1,0:T(8,128)(2,1)} %copy-done, ...), custom_call_target="tpu_custom_call" | custom-call | tf_op jit(solution)/shard_map/pallas_call | solution.py:78
  29.1 0.0 copy-start.7
  29.1 0.7 copy-done.7
  29.8 23.6 %all_to_all.15 = f32[64,1,2]{2,1,0:T(1,128)S(1)} all-to-all(f32[64,1,2]{2,1,0:T(1,128)S(1)} %broadcast_in_dim.26), channel_id=1, replica_groups=mesh['dp'=12,'phase'=4,'ctx'=16] {'phase','ctx'}, dimensions={0} | all-to-all | bytes 1024 | tf_op jit(solution)/shard_map/all_to_all | solution.py:93
  53.4 0.1 reduce_sum.18
  53.5 0.5 copy-done.5
  54.0 23.6 %all_to_all.16 = f32[12,1,2]{2,1,0:T(1,128)S(1)} all-to-all(f32[12,1,2]{2,1,0:T(1,128)S(1)} %broadcast_in_dim.28), channel_id=1, replica_groups=mesh['dp'=12,'phase'=4,'ctx'=16] {'dp'}, dimensions={0} | all-to-all | bytes 192 | tf_op jit(solution)/shard_map/all_to_all | solution.py:93
  77.6 0.1 copy.12
  77.7 0.6 fusion
  (5 shorter events, 0.0 us)
Async XLA Ops:
  0.6 0.7 copy-start.6
  2.4 19.1 %copy-start = (bf16[272,256]{1,0:T(8,128)(2,1)}, bf16[272,256]{1,0:T(8,128)(2,1)S(1)}, u32[]{:S(2)}) copy-start(bf16[272,256]{1,0:T(8,128)(2,1)S(1)} %maximum_maximum_fusion.refs_4_) | copy-start | bytes 417796
  2.4 15.6 %collective-permute-start.3 = (bf16[272,256]{1,0:T(8,128)(2,1)S(1)}, bf16[272,256]{1,0:T(8,128)(2,1)S(1)}, u32[]{:S(2)}, u32[]{:S(2)}) collective-permute-start(bf16[272,256]{1,0:T(8,128)(2,1)S(1)} %maximum_maximum_fusion.refs_4_), channel_id=1, source_target_pairs={{0,1},{1,2},{2,3},{3,4},{4,5},{5,6},{6,7},{7,8},{8,9},{9,10},{10,1... | collective-permute-start | bytes 417800 | tf_op jit(solution)/shard_map/ppermute | solution.py:112
  7.0 11.0 %collective-permute-start.2 = (bf16[272,256]{1,0:T(8,128)(2,1)S(1)}, bf16[272,256]{1,0:T(8,128)(2,1)S(1)}, u32[]{:S(2)}, u32[]{:S(2)}) collective-permute-start(bf16[272,256]{1,0:T(8,128)(2,1)S(1)} %maximum_maximum_fusion.refs_4_), channel_id=1, source_target_pairs={{0,2},{1,3},{2,4},{3,5},{4,6},{5,7},{6,8},{7,9},{8,10},{9,11},{10,... | collective-permute-start | bytes 417800 | tf_op jit(solution)/shard_map/ppermute | solution.py:112
  10.2 7.8 %collective-permute-start.1 = (bf16[272,256]{1,0:T(8,128)(2,1)S(1)}, bf16[272,256]{1,0:T(8,128)(2,1)S(1)}, u32[]{:S(2)}, u32[]{:S(2)}) collective-permute-start(bf16[272,256]{1,0:T(8,128)(2,1)S(1)} %maximum_maximum_fusion.refs_4_), channel_id=1, source_target_pairs={{0,3},{1,4},{2,5},{3,6},{4,7},{5,8},{6,9},{7,10},{8,11},{9,12},{10... | collective-permute-start | bytes 417800 | tf_op jit(solution)/shard_map/ppermute | solution.py:112
  13.4 8.0 %collective-permute-start = (bf16[272,256]{1,0:T(8,128)(2,1)S(1)}, bf16[272,256]{1,0:T(8,128)(2,1)S(1)}, u32[]{:S(2)}, u32[]{:S(2)}) collective-permute-start(bf16[272,256]{1,0:T(8,128)(2,1)S(1)} %maximum_maximum_fusion.refs_4_), channel_id=1, source_target_pairs={{0,4},{1,5},{2,6},{3,7},{4,8},{5,9},{6,10},{7,11},{8,12},{9,13},{1... | collective-permute-start | bytes 417800 | tf_op jit(solution)/shard_map/ppermute | solution.py:112
  18.0 3.5 %copy-start.1 = (bf16[272,256]{1,0:T(8,128)(2,1)}, bf16[272,256]{1,0:T(8,128)(2,1)S(1)}, u32[]{:S(2)}) copy-start(bf16[272,256]{1,0:T(8,128)(2,1)S(1)} %collective-permute-done.3.refs_3_) | copy-start | bytes 417796
  18.0 3.5 %copy-start.2 = (bf16[272,256]{1,0:T(8,128)(2,1)}, bf16[272,256]{1,0:T(8,128)(2,1)S(1)}, u32[]{:S(2)}) copy-start(bf16[272,256]{1,0:T(8,128)(2,1)S(1)} %collective-permute-done.2.refs_2_) | copy-start | bytes 417796
  18.0 3.5 %copy-start.3 = (bf16[272,256]{1,0:T(8,128)(2,1)}, bf16[272,256]{1,0:T(8,128)(2,1)S(1)}, u32[]{:S(2)}) copy-start(bf16[272,256]{1,0:T(8,128)(2,1)S(1)} %collective-permute-done.1.refs_1_) | copy-start | bytes 417796
  21.5 0.7 copy-start.4
  29.1 0.7 copy-start.7
  53.5 0.5 copy-start.5

commit v9 on v8

--- a/solution.py
+++ b/solution.py
@@ -32,27 +32,46 @@
         allow = (kpos <= qpos) & (kpos >= 0) & (kseg == qseg)
         biases.append(jnp.where(allow, 0.0, MASKED))
     scale = 1.0 / jnp.sqrt(jnp.float32(hd))
+    merge = npieces > 1 and (npieces - 1) * tok >= MAX_SEGMENT
+    if merge:
+        tri = lax.broadcasted_iota(jnp.int32, (tok, tok), 1) <= lax.broadcasted_iota(jnp.int32, (tok, tok), 0)
+        chunk_bias = [jnp.where(tri, biases[-1], biases[0])] + biases[1:-1]
+    else:
+        chunk_bias = biases
     score = jnp.zeros((tok, 1), jnp.float32)
     for h in range(width // hd):
         cols = pl.ds(h * hd, hd)
         qh = q_ref[:, cols]
-        scs = []
-        for i, p_ref in enumerate(pieces):
-            sc = lax.dot_general(
+        raw = [
+            lax.dot_general(
                 qh, p_ref[pl.ds(0, tok), pl.ds(0, hd)], (((1,), (1,)), ((), ())),
                 preferred_element_type=jnp.float32,
             )
-            scs.append(sc * scale + biases[i])
+            for p_ref in pieces
+        ]
+        if merge:
+            raw = [jnp.where(tri, raw[-1], raw[0])] + raw[1:-1]
+        scs = [r * scale + b for r, b in zip(raw, chunk_bias)]
         top = scs[0].max(axis=1, keepdims=True)
         for sc in scs[1:]:
             top = jnp.maximum(top, sc.max(axis=1, keepdims=True))
         total = jnp.zeros((tok, 1), jnp.float32)
         acc = jnp.zeros((tok, hd), jnp.float32)
-        for i, p_ref in enumerate(pieces):
-            prob = jnp.exp(scs[i] - top)
+        for i, sc in enumerate(scs):
+            prob = jnp.exp(sc - top)
             total = total + jnp.sum(prob, axis=1, keepdims=True)
+            if merge and i == 0:
+                own = jnp.where(tri, prob, 0.0)
+                acc = acc + jnp.dot(
+                    own.astype(jnp.bfloat16), pieces[-1][pl.ds(0, tok), pl.ds(hd, hd)],
+                    preferred_element_type=jnp.float32,
+                )
+                prob = prob - own
+                src_ref = pieces[0]
+            else:
+                src_ref = pieces[i] if not merge else pieces[i]
             acc = acc + jnp.dot(
-                prob.astype(jnp.bfloat16), p_ref[pl.ds(0, tok), pl.ds(hd, hd)],
+                prob.astype(jnp.bfloat16), src_ref[pl.ds(0, tok), pl.ds(hd, hd)],
                 preferred_element_type=jnp.float32,
             )
         full = acc / total

time: 80.5 us -> 80.3 us (level)
  no operation moved by 1% of the time
where the time goes in v9:
time: 80.3 us; the launch traced here: 79.9 us
  blocking collectives  47.2 us (59%)
  starting transfers between devices  15.5 us (19%)
  Pallas kernels  6.8 us (8%)
  waiting for transfers between devices  3.45 us (4%)
  between operations  2.55 us (3%)
  other arithmetic  2.37 us (3%)
  local copies, waits for them, and re-layouts  2 us (2%)
    all_to_all x2, blocking collectives, gathered(): return lax.all_to_all(copies, axes, 0, 0, tiled=False)  47.2 us
    ppermute x4, starting transfers between devices, per_device(): pieces.append(lax.ppermute(packed, 'ctx', pairs))  15.5 us
    pallas_call x1, Pallas kernels, attend(): pl.pallas_call(attend_kernel, grid_spec=grid_spec, out_shape=[jax.ShapeDt...  6.8 us
    ppermute x4, waiting for transfers between devices, per_device(): pieces.append(lax.ppermute(packed, 'ctx', pairs))  3.45 us
    unnamed x16, local copies, waits for them, and re-layouts  1.8 us
  transfers between devices with their start and end apart: 4, of which 1 were waited for; matrix products, arithmetic and copies ran while one was open for 0% of the time, Pallas kernels for 0%

profile of v9, /device:TPU:1, one launch (start us, length us, event | category | flops | bytes accessed | tf_op | source)
XLA Modules:
  0.0 79.9 jit_solution(8224048537672349921)
XLA Ops:
  0.6 0.0 copy-start.6
  0.6 0.7 convert.6
  1.3 0.0 copy-done.6
  1.3 0.1 pad.4.clone
  1.4 1.0 %maximum_maximum_fusion.refs_4_ = bf16[272,256]{1,0:T(8,128)(2,1)S(1)} fusion(bf16[1,256]{1,0:T(2,128)(2,1)S(1)} %convert.7, bf16[1,256]{1,0:T(2,128)(2,1)S(1)} %convert.6, bf16[256,128]{1,0:T(8,128)(2,1)} %bitcast.26, bf16[256,128]{1,0:T(8,128)(2,1)} %bitcast.27, bf16[272]{0:T(512)(128)(2,1)S(1)} %pad.4.clone), kind=kLoop, calls=%fused_computation | loop fusion | flops 696320 | bytes 271904 | tf_op jit(solution)/shard_map/concatenate | solution.py:127
  2.4 0.0 copy-start
  2.4 4.6 %collective-permute-start.3 = (bf16[272,256]{1,0:T(8,128)(2,1)S(1)}, bf16[272,256]{1,0:T(8,128)(2,1)S(1)}, u32[]{:S(2)}, u32[]{:S(2)}) collective-permute-start(bf16[272,256]{1,0:T(8,128)(2,1)S(1)} %maximum_maximum_fusion.refs_4_), channel_id=1, source_target_pairs={{0,1},{1,2},{2,3},{3,4},{4,5},{5,6},{6,7},{7,8},{8,9},{9,10},{10,1... | collective-permute-start | bytes 417800 | tf_op jit(solution)/shard_map/ppermute | solution.py:131
  7.0 3.2 %collective-permute-start.2 = (bf16[272,256]{1,0:T(8,128)(2,1)S(1)}, bf16[272,256]{1,0:T(8,128)(2,1)S(1)}, u32[]{:S(2)}, u32[]{:S(2)}) collective-permute-start(bf16[272,256]{1,0:T(8,128)(2,1)S(1)} %maximum_maximum_fusion.refs_4_), channel_id=1, source_target_pairs={{0,2},{1,3},{2,4},{3,5},{4,6},{5,7},{6,8},{7,9},{8,10},{9,11},{10,... | collective-permute-start | bytes 417800 | tf_op jit(solution)/shard_map/ppermute | solution.py:131
  10.2 3.2 %collective-permute-start.1 = (bf16[272,256]{1,0:T(8,128)(2,1)S(1)}, bf16[272,256]{1,0:T(8,128)(2,1)S(1)}, u32[]{:S(2)}, u32[]{:S(2)}) collective-permute-start(bf16[272,256]{1,0:T(8,128)(2,1)S(1)} %maximum_maximum_fusion.refs_4_), channel_id=1, source_target_pairs={{0,3},{1,4},{2,5},{3,6},{4,7},{5,8},{6,9},{7,10},{8,11},{9,12},{10... | collective-permute-start | bytes 417800 | tf_op jit(solution)/shard_map/ppermute | solution.py:131
  13.4 4.5 %collective-permute-start = (bf16[272,256]{1,0:T(8,128)(2,1)S(1)}, bf16[272,256]{1,0:T(8,128)(2,1)S(1)}, u32[]{:S(2)}, u32[]{:S(2)}) collective-permute-start(bf16[272,256]{1,0:T(8,128)(2,1)S(1)} %maximum_maximum_fusion.refs_4_), channel_id=1, source_target_pairs={{0,4},{1,5},{2,6},{3,7},{4,8},{5,9},{6,10},{7,11},{8,12},{9,13},{1... | collective-permute-start | bytes 417800 | tf_op jit(solution)/shard_map/ppermute | solution.py:131
  18.0 0.0 collective-permute-done.3.refs_3_
  18.0 0.0 copy-start.1
  18.0 0.0 collective-permute-done.2.refs_2_
  18.0 0.0 copy-start.2
  18.0 0.0 collective-permute-done.1.refs_1_
  18.0 0.0 copy-start.3
  18.0 3.4 %collective-permute-done.refs_0_ = bf16[272,256]{1,0:T(8,128)(2,1)S(1)} collective-permute-done((bf16[272,256]{1,0:T(8,128)(2,1)S(1)}, bf16[272,256]{1,0:T(8,128)(2,1)S(1)}, u32[]{:S(2)}, u32[]{:S(2)}) %collective-permute-start) | collective-permute-done | bytes 139296 | tf_op jit(solution)/shard_map/ppermute | solution.py:131
  21.5 0.0 copy-start.4
  21.5 0.0 copy-done
  21.5 0.0 copy-done.1
  21.5 0.0 copy-done.2
  21.5 0.0 copy-done.3
  21.5 0.6 copy-done.4
  22.1 6.8 %shard_map.85 = (bf16[256,1024]{1,0:T(8,128)(2,1)}, f32[1,2]{1,0:T(1,128)}) custom-call(s32[1]{0:T(128)} %bitcast.here_ref, bf16[272,256]{1,0:T(8,128)(2,1)} %copy-done.4, bf16[272,256]{1,0:T(8,128)(2,1)} %copy-done.3, bf16[272,256]{1,0:T(8,128)(2,1)} %copy-done.2, bf16[272,256]{1,0:T(8,128)(2,1)} %copy-done.1, bf16[272,256]{1,0:T(8,128)(2,1)} %copy-done, ...), custom_call_target="tpu_custom_call" | custom-call | tf_op jit(solution)/shard_map/pallas_call | solution.py:97
  28.9 0.0 copy-start.7
  28.9 0.7 copy-done.7
  29.6 23.6 %all_to_all.15 = f32[64,1,2]{2,1,0:T(1,128)S(1)} all-to-all(f32[64,1,2]{2,1,0:T(1,128)S(1)} %broadcast_in_dim.26), channel_id=1, replica_groups=mesh['dp'=12,'phase'=4,'ctx'=16] {'phase','ctx'}, dimensions={0} | all-to-all | bytes 1024 | tf_op jit(solution)/shard_map/all_to_all | solution.py:112
  53.2 0.1 reduce_sum.18
  53.3 0.5 copy-done.5
  53.8 23.6 %all_to_all.16 = f32[12,1,2]{2,1,0:T(1,128)S(1)} all-to-all(f32[12,1,2]{2,1,0:T(1,128)S(1)} %broadcast_in_dim.28), channel_id=1, replica_groups=mesh['dp'=12,'phase'=4,'ctx'=16] {'dp'}, dimensions={0} | all-to-all | bytes 192 | tf_op jit(solution)/shard_map/all_to_all | solution.py:112
  77.4 0.1 copy.12
  77.5 0.6 fusion
  (5 shorter events, 0.0 us)
Async XLA Ops:
  0.6 0.7 copy-start.6
  2.4 19.1 %copy-start = (bf16[272,256]{1,0:T(8,128)(2,1)}, bf16[272,256]{1,0:T(8,128)(2,1)S(1)}, u32[]{:S(2)}) copy-start(bf16[272,256]{1,0:T(8,128)(2,1)S(1)} %maximum_maximum_fusion.refs_4_) | copy-start | bytes 417796
  2.4 15.6 %collective-permute-start.3 = (bf16[272,256]{1,0:T(8,128)(2,1)S(1)}, bf16[272,256]{1,0:T(8,128)(2,1)S(1)}, u32[]{:S(2)}, u32[]{:S(2)}) collective-permute-start(bf16[272,256]{1,0:T(8,128)(2,1)S(1)} %maximum_maximum_fusion.refs_4_), channel_id=1, source_target_pairs={{0,1},{1,2},{2,3},{3,4},{4,5},{5,6},{6,7},{7,8},{8,9},{9,10},{10,1... | collective-permute-start | bytes 417800 | tf_op jit(solution)/shard_map/ppermute | solution.py:131
  7.0 11.0 %collective-permute-start.2 = (bf16[272,256]{1,0:T(8,128)(2,1)S(1)}, bf16[272,256]{1,0:T(8,128)(2,1)S(1)}, u32[]{:S(2)}, u32[]{:S(2)}) collective-permute-start(bf16[272,256]{1,0:T(8,128)(2,1)S(1)} %maximum_maximum_fusion.refs_4_), channel_id=1, source_target_pairs={{0,2},{1,3},{2,4},{3,5},{4,6},{5,7},{6,8},{7,9},{8,10},{9,11},{10,... | collective-permute-start | bytes 417800 | tf_op jit(solution)/shard_map/ppermute | solution.py:131
  10.2 7.8 %collective-permute-start.1 = (bf16[272,256]{1,0:T(8,128)(2,1)S(1)}, bf16[272,256]{1,0:T(8,128)(2,1)S(1)}, u32[]{:S(2)}, u32[]{:S(2)}) collective-permute-start(bf16[272,256]{1,0:T(8,128)(2,1)S(1)} %maximum_maximum_fusion.refs_4_), channel_id=1, source_target_pairs={{0,3},{1,4},{2,5},{3,6},{4,7},{5,8},{6,9},{7,10},{8,11},{9,12},{10... | collective-permute-start | bytes 417800 | tf_op jit(solution)/shard_map/ppermute | solution.py:131
  13.4 8.0 %collective-permute-start = (bf16[272,256]{1,0:T(8,128)(2,1)S(1)}, bf16[272,256]{1,0:T(8,128)(2,1)S(1)}, u32[]{:S(2)}, u32[]{:S(2)}) collective-permute-start(bf16[272,256]{1,0:T(8,128)(2,1)S(1)} %maximum_maximum_fusion.refs_4_), channel_id=1, source_target_pairs={{0,4},{1,5},{2,6},{3,7},{4,8},{5,9},{6,10},{7,11},{8,12},{9,13},{1... | collective-permute-start | bytes 417800 | tf_op jit(solution)/shard_map/ppermute | solution.py:131
  18.0 3.5 %copy-start.1 = (bf16[272,256]{1,0:T(8,128)(2,1)}, bf16[272,256]{1,0:T(8,128)(2,1)S(1)}, u32[]{:S(2)}) copy-start(bf16[272,256]{1,0:T(8,128)(2,1)S(1)} %collective-permute-done.3.refs_3_) | copy-start | bytes 417796
  18.0 3.5 %copy-start.2 = (bf16[272,256]{1,0:T(8,128)(2,1)}, bf16[272,256]{1,0:T(8,128)(2,1)S(1)}, u32[]{:S(2)}) copy-start(bf16[272,256]{1,0:T(8,128)(2,1)S(1)} %collective-permute-done.2.refs_2_) | copy-start | bytes 417796
  18.0 3.5 %copy-start.3 = (bf16[272,256]{1,0:T(8,128)(2,1)}, bf16[272,256]{1,0:T(8,128)(2,1)S(1)}, u32[]{:S(2)}) copy-start(bf16[272,256]{1,0:T(8,128)(2,1)S(1)} %collective-permute-done.1.refs_1_) | copy-start | bytes 417796
  21.5 0.7 copy-start.4
  28.9 0.7 copy-start.7
  53.3 0.5 copy-start.5
